TPU v7x, 1024 devices: a whole 4x4x32 slice. The times are simulated.
1024 devices in a mesh: ctx: 16 (over y, x), tp: 64 (over z, core).
Axes of the slice: x: 4, y: 4, z: 32, core: 2. Of those that a mesh axis runs over, the one named last changes fastest.
Arguments:
- tokens: bfloat16 [2048, 16384], P(None, 'ctx'), may hold values from -4 to 4
- wq: bfloat16 [16384, 16384], P('ctx', 'tp'), may hold values from -0.046875 to 0.046875
- wk: bfloat16 [16384, 1024], P('ctx', 'tp'), may hold values from -0.046875 to 0.046875
- wv: bfloat16 [16384, 1024], P('ctx', 'tp'), may hold values from -0.046875 to 0.046875
- doc_len: int32 [64], replicated, may hold values from 1 to 189, as said below
- doc_shard: int32 [64], replicated, may hold values from 0 to 15, as said below
- doc_slot: int32 [64], replicated, may hold values from 0 to 191, as said below
Outputs:
- attended: bfloat16 [3072, 16384], P('ctx', 'tp')
Inputs may be any that keep to these rules, and one draw needn't show every extreme that they name: `doc_len`: documents lie in the packed sequence in index order and their lengths sum to 2048; in every draw some document has length 189. `doc_shard`: each shard holds exactly 4 documents whose lengths sum to at most 192; in every draw some shard holds exactly 192 tokens. The documents of one shard take disjoint runs of slots doc_slot to doc_slot + doc_len - 1, filling the slots from 0 without gaps; in every draw some document starts at slot 191.
All inputs are finite; a program needn't handle non-finite values.
Results may differ from a plain program's by a relative error of at most 0.035.
Values may be sent and summed in bfloat16 or wider, within the bound.
No kernel may reach another device: no remote copies, remote signals or barrier semaphores. Data moves between devices by JAX's collectives and lax.ppermute only.
A program may use at most 32 MiB of HBM per device.

v0:
```python
import jax
import jax.numpy as jnp
from jax import lax
from jax.sharding import PartitionSpec as P

HEAD_SIZE = 128


rope_base = 500000.0


def partner(shard, axis, apart):
    return lax.ppermute(shard, axis, [(i, i ^ 1 << apart) for i in range(lax.axis_size(axis))])


def slot_layout(doc_len, doc_shard, doc_slot, tokens_total, capacity, slot_total):
    ends = jnp.cumsum(doc_len)
    starts = ends - doc_len
    token_ids = jnp.arange(tokens_total, dtype=jnp.int32)
    inside = (token_ids[:, None] >= starts[None, :]) & (token_ids[:, None] < ends[None, :])
    doc_ids = jnp.arange(doc_len.shape[0], dtype=jnp.int32)
    doc_of = jnp.sum(jnp.where(inside, doc_ids[None, :], 0), axis=1)
    first = jnp.sum(jnp.where(inside, starts[None, :], 0), axis=1)
    anchor = doc_shard * capacity + doc_slot
    base = jnp.sum(jnp.where(inside, anchor[None, :], 0), axis=1)
    position = token_ids - first
    target = base + position
    slot_ids = jnp.arange(slot_total, dtype=jnp.int32)
    source = jnp.zeros((slot_total,), jnp.int32).at[target].set(token_ids)
    filled = jnp.zeros((slot_total,), jnp.int32).at[target].set(1)
    slot_doc = jnp.zeros((slot_total,), jnp.int32).at[target].set(doc_of)
    slot_doc = jnp.where(filled == 1, slot_doc, -1 - slot_ids)
    slot_position_index = jnp.zeros((slot_total,), jnp.int32).at[target].set(position)
    return (source, filled, slot_doc, slot_position_index)


def apply_rotary(values, positions):
    head_dim = values.shape[-1]
    half = head_dim // 2
    freq = jnp.power(
        jnp.float32(rope_base), -jnp.arange(half, dtype=jnp.float32) * (2.0 / head_dim)
    )
    angle = positions.astype(jnp.float32)[:, None] * freq[None, :]
    cosine = jnp.cos(angle)[:, None, :]
    sine = jnp.sin(angle)[:, None, :]
    lower = values[..., :half]
    upper = values[..., half:]
    return jnp.concatenate([lower * cosine - upper * sine, upper * cosine + lower * sine], axis=-1)


def attend(query_matrix, key, value_matrix, slot_doc, slot_position_index):
    scale = query_matrix.shape[-1] ** (-0.5)
    scores = (
        jnp.einsum("qgjd,kgd->gjqk", query_matrix, key, preferred_element_type=jnp.float32) * scale
    )
    allowed = (slot_doc[:, None] == slot_doc[None, :]) & (
        slot_position_index[None, :] <= slot_position_index[:, None]
    )
    scores = jnp.where(allowed[None, None], scores, -jnp.inf)
    peak = jnp.max(scores, axis=-1, keepdims=True)
    expo = jnp.exp(scores - peak)
    total = jnp.sum(expo, axis=-1)
    weights = expo.astype(jnp.bfloat16)
    mixed = jnp.einsum("gjqk,kgd->qgjd", weights, value_matrix, preferred_element_type=jnp.float32)
    result = mixed / jnp.transpose(total, (2, 0, 1))[..., None]
    return result.astype(jnp.bfloat16)


def body(tokens, wq, wk, wv, doc_len, doc_shard, doc_slot):
    shards = lax.axis_size("ctx")
    total_tokens = tokens.shape[0]
    per_shard = total_tokens // shards
    capacity = per_shard + per_shard // 2
    slot_total = capacity * shards
    source, filled, slot_doc, slot_position_index = slot_layout(
        doc_len, doc_shard, doc_slot, total_tokens, capacity, slot_total
    )
    joined = jnp.concatenate([wq, wk, wv], axis=1)
    q_cols = wq.shape[1]
    key_value_columns = wk.shape[1]
    picked = jnp.take(tokens, source, axis=0)
    partial_rows = jnp.dot(picked, joined, preferred_element_type=jnp.float32)
    summed = lax.psum_scatter(
        jnp.where(filled[:, None] == 1, partial_rows, jnp.float32(0.0)).astype(jnp.bfloat16),
        "ctx",
        scatter_dimension=0,
        tiled=True,
    ).astype(jnp.float32)
    shard = lax.axis_index("ctx")
    my_doc = lax.dynamic_slice_in_dim(slot_doc, shard * capacity, capacity)
    my_pos = lax.dynamic_slice_in_dim(slot_position_index, shard * capacity, capacity)
    heads_here = q_cols // HEAD_SIZE
    query_matrix = apply_rotary(
        summed[:, :q_cols].reshape(capacity, heads_here, HEAD_SIZE), my_pos
    ).astype(jnp.bfloat16)
    piece = jnp.stack(
        [summed[:, q_cols : q_cols + key_value_columns], summed[:, q_cols + key_value_columns :]],
        axis=0,
    ).astype(jnp.bfloat16)
    members = HEAD_SIZE // key_value_columns
    member = lax.axis_index("tp") % members
    for bit in range(members.bit_length() - 1):
        other = partner(piece, "tp", bit)
        upper_bit = member // 2**bit % 2
        lower_part = jnp.where(upper_bit == 0, piece, other)
        upper_part = jnp.where(upper_bit == 0, other, piece)
        piece = jnp.concatenate([lower_part, upper_part], axis=2)
    key_unrotated = lax.optimization_barrier(piece[0])
    value_matrix = piece[1]
    key = apply_rotary(key_unrotated.astype(jnp.float32)[:, None, :], my_pos).astype(jnp.bfloat16)
    result = attend(
        query_matrix.reshape(capacity, 1, heads_here, HEAD_SIZE),
        key,
        value_matrix[:, None, :],
        my_doc,
        my_pos,
    )
    return result.reshape(capacity, heads_here * HEAD_SIZE)


def solution(mesh):
    return jax.shard_map(
        body,
        mesh=mesh,
        in_specs=(P(None, "ctx"), P("ctx", "tp"), P("ctx", "tp"), P("ctx", "tp"), P(), P(), P()),
        out_specs=P("ctx", "tp"),
        check_vma=False,
    )
```

profile of v0, /device:TPU:1, one launch (start us, length us, event | category | flops | bytes accessed | tf_op | source)
XLA Modules:
  0.0 199.6 jit_solution(3623874748300516332)
XLA Ops:
  6.5 0.0 reduce-scatter.2.cloned.1.call-start
  6.5 0.7 copy.33
  7.3 0.1 reduce-window.8
  7.4 0.1 reduce.2
  7.5 0.7 sub.45
  8.2 0.7 multiply_add_fusion
  8.8 0.3 select_reduce_fusion
  9.2 8.1 %scatter_custom_fusion.1 = s32[3072]{0:T(1024)S(1)} fusion(s32[2048]{0:T(1024)S(1)} %bitcast.57, s32[2048]{0:T(1024)S(1)} %iota.27, s32[]{:T(128)} %constant.92.clone.1), kind=kCustom, calls=%fused_computation.85 | custom fusion | bytes 12292 | tf_op jit(solution)/shard_map/scatter | solution.py:29
  17.3 8.1 %scatter_custom_fusion = s32[3072]{0:T(1024)S(1)} fusion(s32[2048]{0:T(1024)S(1)} %bitcast.58, s32[2048]{0:T(1024)S(1)} %broadcast.166, s32[]{:T(128)} %constant.92.clone.1), kind=kCustom, calls=%fused_computation.87 | custom fusion | bytes 12292 | tf_op jit(solution)/shard_map/scatter | solution.py:30
  25.4 0.9 copy.35
  26.3 0.9 copy.34
  27.3 0.0 copy-start
  27.3 18.7 %gather_fusion = bf16[3072,1024]{1,0:T(8,128)(2,1)} fusion(bf16[2048,1024]{1,0:T(8,128)(2,1)} %param.7, s32[3072]{0:T(1024)S(1)} %fusion.40), kind=kCustom, calls=%fused_computation | custom fusion | bytes 12595200 | tf_op jit(solution)/shard_map/jit(_take)/gather | solution.py:81
  46.0 0.0 copy-done
  46.0 7.8 %select_convert_fusion = bf16[3072,288]{1,0:T(8,128)(2,1)} fusion(bf16[3072,1024]{1,0:T(8,128)(2,1)} %gather_fusion, pred[3072]{0:T(1024)(128)(4,1)S(1)} %get-tuple-element.28, pred[3072]{0:T(1024)(128)(4,1)S(1)} %get-tuple-element.29, bf16[1024,16]{1,0:T(8,128)(2,1)S(1)} %copy.35, bf16[1024,16]{1,0:T(8,128)(2,1)S(1)} %copy.34, bf16[1024,256]{1,0:T(8,128)(2,1)S(1)} %copy-done), kind=kOutput, calls=%fused_computation.8 | convolution fusion | flops 1818624000 | bytes 8656896 | tf_op jit(solution)/shard_map/dot_general | solution.py:82
  53.8 0.0 reduce-scatter.2.cloned.1.call-update
  53.9 8.1 %scatter_custom_fusion.3 = s32[3072]{0:T(1024)S(1)} fusion(s32[2048]{0:T(1024)S(1)} %bitcast.59, s32[2048]{0:T(1024)S(1)} %iota_subtract_fusion, s32[]{:T(128)} %constant.92.clone.1), kind=kCustom, calls=%fused_computation.81 | custom fusion | bytes 12292 | tf_op jit(solution)/shard_map/scatter | solution.py:33
  62.0 8.1 %scatter_custom_fusion.2 = s32[3072]{0:T(1024)S(1)} fusion(s32[2048]{0:T(1024)S(1)} %bitcast.60, s32[2048]{0:T(1024)S(1)} %get-tuple-element.5, s32[]{:T(128)} %constant.92.clone.1), kind=kCustom, calls=%fused_computation.83 | custom fusion | bytes 12292 | tf_op jit(solution)/shard_map/scatter | solution.py:31
  70.1 0.1 dynamic-slice_select_fusion
  70.2 0.1 fusion.53
  70.3 0.1 compare_and_fusion
  70.4 0.4 multiply_cosine_fusion
  70.9 100.4 %reduce-scatter.2.cloned.1.call-done = bf16[192,288]{1,0:T(8,128)(2,1)} async-done(((bf16[3072,288]{1,0:T(8,128)(2,1)}), bf16[192,288]{1,0:T(8,128)(2,1)}) %reduce-scatter.2.cloned.1.call-update) | async-done | bytes 110608 | tf_op jit(solution)/shard_map/reduce_scatter | solution.py:83
  171.3 1.0 slice_bitcast_fusion.1
  172.3 0.1 copy.37
  172.3 0.1 copy.36
  172.4 4.3 %collective-permute-start = (bf16[2,192,16]{1,2,0:T(8,128)(2,1)S(1)}, bf16[2,192,16]{1,2,0:T(8,128)(2,1)S(1)}, u32[]{:S(2)}, u32[]{:S(2)}) collective-permute-start(bf16[2,192,16]{1,2,0:T(8,128)(2,1)S(1)} %pad_maximum_fusion.3), channel_id=1, source_target_pairs={{0,1},{1,0},{2,3},{3,2},{4,5},{5,4},{6,7},{7,6},{8,9},{9,8},{10,11... | collective-permute-start | bytes 36872 | tf_op jit(solution)/shard_map/ppermute | solution.py:13
  176.8 0.9 slice_convert_fusion
  177.7 0.1 reshape.273
  177.8 0.0 collective-permute-done
  177.8 0.1 copy.39
  178.0 3.2 %collective-permute-start.1 = (bf16[2,192,32]{2,1,0:T(8,128)(2,1)S(1)}, bf16[2,192,32]{2,1,0:T(8,128)(2,1)S(1)}, u32[]{:S(2)}, u32[]{:S(2)}) collective-permute-start(bf16[2,192,32]{2,1,0:T(8,128)(2,1)S(1)} %copy.39), channel_id=1, source_target_pairs={{0,2},{1,3},{2,0},{3,1},{4,6},{5,7},{6,4},{7,5},{8,10},{9,11},{10,... | collective-permute-start | bytes 73736 | tf_op jit(solution)/shard_map/ppermute | solution.py:13
  181.1 0.3 fusion.54
  181.4 2.7 %collective-permute-done.1 = bf16[2,192,32]{2,1,0:T(8,128)(2,1)S(1)} collective-permute-done((bf16[2,192,32]{2,1,0:T(8,128)(2,1)S(1)}, bf16[2,192,32]{2,1,0:T(8,128)(2,1)S(1)}, u32[]{:S(2)}, u32[]{:S(2)}) %collective-permute-start.1) | collective-permute-done | bytes 24608 | tf_op jit(solution)/shard_map/ppermute | solution.py:13
  184.1 0.1 pad_maximum_fusion
  184.2 4.2 %collective-permute-start.2 = (bf16[2,192,64]{2,1,0:T(8,128)(2,1)S(1)}, bf16[2,192,64]{2,1,0:T(8,128)(2,1)S(1)}, u32[]{:S(2)}, u32[]{:S(2)}) collective-permute-start(bf16[2,192,64]{2,1,0:T(8,128)(2,1)S(1)} %pad_maximum_fusion), channel_id=1, source_target_pairs={{0,4},{1,5},{2,6},{3,7},{4,0},{5,1},{6,2},{7,3},{8,12},{9,13},{10,... | collective-permute-start | bytes 147464 | tf_op jit(solution)/shard_map/ppermute | solution.py:13
  188.4 0.1 subtract_convert_fusion
  188.5 2.0 %collective-permute-done.2 = bf16[2,192,64]{2,1,0:T(8,128)(2,1)S(1)} collective-permute-done((bf16[2,192,64]{2,1,0:T(8,128)(2,1)S(1)}, bf16[2,192,64]{2,1,0:T(8,128)(2,1)S(1)}, u32[]{:S(2)}, u32[]{:S(2)}) %collective-permute-start.2) | collective-permute-done | bytes 49184 | tf_op jit(solution)/shard_map/ppermute | solution.py:13
  190.5 0.1 broadcast_select_fusion.3
  190.6 0.1 fusion.35
  190.8 0.5 fusion.39
  191.2 0.3 fusion.55
  191.5 0.1 fusion.16
  191.6 0.3 fusion.9
  191.9 0.1 copy.44
  192.1 0.7 copy.54
  (12 shorter events, 0.1 us)
Async XLA Ops:
  6.5 164.8 %reduce-scatter.2.cloned.1.call-start = ((), (), s32[]{:S(2)}) async-start(), calls=%async_computation.1 | async-start | bytes 2506752 | tf_op jit(solution)/shard_map/reduce_scatter | solution.py:83
  27.3 18.8 %copy-start = (bf16[1024,256]{1,0:T(8,128)(2,1)S(1)}, bf16[1024,256]{1,0:T(8,128)(2,1)}, u32[]{:S(2)}) copy-start(bf16[1024,256]{1,0:T(8,128)(2,1)} %param.8) | copy-start | bytes 1572868
  172.4 5.4 %collective-permute-start = (bf16[2,192,16]{1,2,0:T(8,128)(2,1)S(1)}, bf16[2,192,16]{1,2,0:T(8,128)(2,1)S(1)}, u32[]{:S(2)}, u32[]{:S(2)}) collective-permute-start(bf16[2,192,16]{1,2,0:T(8,128)(2,1)S(1)} %pad_maximum_fusion.3), channel_id=1, source_target_pairs={{0,1},{1,0},{2,3},{3,2},{4,5},{5,4},{6,7},{7,6},{8,9},{9,8},{10,11... | collective-permute-start | bytes 36872 | tf_op jit(solution)/shard_map/ppermute | solution.py:13
  178.0 6.2 %collective-permute-start.1 = (bf16[2,192,32]{2,1,0:T(8,128)(2,1)S(1)}, bf16[2,192,32]{2,1,0:T(8,128)(2,1)S(1)}, u32[]{:S(2)}, u32[]{:S(2)}) collective-permute-start(bf16[2,192,32]{2,1,0:T(8,128)(2,1)S(1)} %copy.39), channel_id=1, source_target_pairs={{0,2},{1,3},{2,0},{3,1},{4,6},{5,7},{6,4},{7,5},{8,10},{9,11},{10,... | collective-permute-start | bytes 73736 | tf_op jit(solution)/shard_map/ppermute | solution.py:13
  184.2 6.3 %collective-permute-start.2 = (bf16[2,192,64]{2,1,0:T(8,128)(2,1)S(1)}, bf16[2,192,64]{2,1,0:T(8,128)(2,1)S(1)}, u32[]{:S(2)}, u32[]{:S(2)}) collective-permute-start(bf16[2,192,64]{2,1,0:T(8,128)(2,1)S(1)} %pad_maximum_fusion), channel_id=1, source_target_pairs={{0,4},{1,5},{2,6},{3,7},{4,0},{5,1},{6,2},{7,3},{8,12},{9,13},{10,... | collective-permute-start | bytes 147464 | tf_op jit(solution)/shard_map/ppermute | solution.py:13
Sparse Core Ops, SparseCore 0:
  54.0 117.2 reduce-scatter.1
where the time goes:
time: 202 us; the launch traced here: 200 us
  waiting for transfers between devices  105 us (52%)
  local copies, waits for them, and re-layouts  55.9 us (28%)
  between operations  13.8 us (7%)
  starting transfers between devices  11.6 us (6%)
  matrix products  8.44 us (4%)
  other arithmetic  4.55 us (2%)
    reduce_scatter x1, waiting for transfers between devices, body(): lax.psum_scatter(jnp.where(filled[:, None] == 1, partial_rows, jnp.float3...  100 us
    gather x1, local copies, waits for them, and re-layouts, body(): picked = jnp.take(tokens, source, axis=0)  18.7 us
    ppermute x3, starting transfers between devices, partner(): lax.ppermute(shard, axis, [(i, i ^ 1 << apart) for i in range(lax.axis_si...  11.6 us
    scatter x1, local copies, waits for them, and re-layouts, slot_layout(): source = jnp.zeros((slot_total,), jnp.int32).at[target].set(token_ids)  8.06 us
    scatter x1, local copies, waits for them, and re-layouts, slot_layout(): filled = jnp.zeros((slot_total,), jnp.int32).at[target].set(1)  8.06 us
    scatter x1, local copies, waits for them, and re-layouts, slot_layout(): jnp.zeros((slot_total,), jnp.int32).at[target].set(position)  8.06 us
    scatter x1, local copies, waits for them, and re-layouts, slot_layout(): slot_doc = jnp.zeros((slot_total,), jnp.int32).at[target].set(doc_of)  8.06 us
    dot_general x1, matrix products, body(): partial_rows = jnp.dot(picked, joined, preferred_element_type=jnp.float32)  7.81 us
  transfers between devices with their start and end apart: 4, of which 3 were waited for; matrix products, arithmetic and copies ran while one was open for 9% of the time, Pallas kernels for 0%

commit v1 on v0

v1 whole, which is shorter than its diff:
```python
import jax
import jax.numpy as jnp
from jax import lax
from jax.sharding import PartitionSpec as P

HEAD_SIZE = 128


rope_base = 500000.0


def slot_table(slot_ids, doc_len, doc_shard, doc_slot, capacity):
    ends = jnp.cumsum(doc_len)
    starts = ends - doc_len
    shard_of = slot_ids // capacity
    local = slot_ids % capacity
    offset = local[:, None] - doc_slot[None, :]
    match = (
        (shard_of[:, None] == doc_shard[None, :]) & (offset >= 0) & (offset < doc_len[None, :])
    )
    filled = jnp.any(match, axis=1)
    position = jnp.sum(jnp.where(match, offset, 0), axis=1)
    source = jnp.sum(jnp.where(match, starts[None, :] + offset, 0), axis=1)
    doc_ids = jnp.arange(doc_len.shape[0], dtype=jnp.int32)
    doc_of = jnp.sum(jnp.where(match, doc_ids[None, :], 0), axis=1)
    slot_doc = jnp.where(filled, doc_of, -1 - slot_ids)
    return (source, filled, slot_doc, position)


def apply_rotary(values, positions):
    head_dim = values.shape[-1]
    half = head_dim // 2
    freq = jnp.power(
        jnp.float32(rope_base), -jnp.arange(half, dtype=jnp.float32) * (2.0 / head_dim)
    )
    angle = positions.astype(jnp.float32)[:, None] * freq[None, :]
    cosine = jnp.cos(angle)[:, None, :]
    sine = jnp.sin(angle)[:, None, :]
    lower = values[..., :half]
    upper = values[..., half:]
    return jnp.concatenate([lower * cosine - upper * sine, upper * cosine + lower * sine], axis=-1)


def attend(query_matrix, key, value_matrix, slot_doc, slot_position_index):
    scale = query_matrix.shape[-1] ** (-0.5)
    scores = (
        jnp.einsum("qgjd,kgd->gjqk", query_matrix, key, preferred_element_type=jnp.float32) * scale
    )
    allowed = (slot_doc[:, None] == slot_doc[None, :]) & (
        slot_position_index[None, :] <= slot_position_index[:, None]
    )
    scores = jnp.where(allowed[None, None], scores, -jnp.inf)
    peak = jnp.max(scores, axis=-1, keepdims=True)
    expo = jnp.exp(scores - peak)
    total = jnp.sum(expo, axis=-1)
    weights = expo.astype(jnp.bfloat16)
    mixed = jnp.einsum("gjqk,kgd->qgjd", weights, value_matrix, preferred_element_type=jnp.float32)
    result = mixed / jnp.transpose(total, (2, 0, 1))[..., None]
    return result.astype(jnp.bfloat16)


def body(tokens, wq, wk, wv, doc_len, doc_shard, doc_slot):
    shards = lax.axis_size("ctx")
    total_tokens = tokens.shape[0]
    per_shard = total_tokens // shards
    capacity = per_shard + per_shard // 2
    slot_total = capacity * shards
    q_cols = wq.shape[1]
    key_value_columns = wk.shape[1]
    members = HEAD_SIZE // key_value_columns
    groups = [
        list(range(g * members, (g + 1) * members))
        for g in range(lax.axis_size("tp") // members)
    ]
    pieces = lax.all_gather(
        jnp.concatenate([wk, wv], axis=1), "tp", axis=0, axis_index_groups=groups
    )
    width = pieces.shape[1]
    key_weights = jnp.transpose(pieces[:, :, :key_value_columns], (1, 0, 2)).reshape(width, HEAD_SIZE)
    value_weights = jnp.transpose(pieces[:, :, key_value_columns:], (1, 0, 2)).reshape(width, HEAD_SIZE)

    source, filled, _, _ = slot_table(
        jnp.arange(slot_total, dtype=jnp.int32), doc_len, doc_shard, doc_slot, capacity
    )
    token_ids = jnp.arange(total_tokens, dtype=jnp.int32)
    placement = ((source[:, None] == token_ids[None, :]) & filled[:, None]).astype(jnp.bfloat16)

    query_term = jnp.dot(tokens, wq, preferred_element_type=jnp.float32).astype(jnp.bfloat16)
    kv_term = jnp.dot(
        tokens, jnp.concatenate([key_weights, value_weights], axis=1), preferred_element_type=jnp.float32
    ).astype(jnp.bfloat16)
    term = jnp.concatenate([query_term, kv_term], axis=1)
    slot_rows = jnp.dot(placement, term, preferred_element_type=jnp.float32).astype(jnp.bfloat16)
    columns = slot_rows.shape[1]
    received = lax.all_to_all(
        slot_rows.reshape(shards, capacity, columns), "ctx", 0, 0, tiled=False
    )
    summed = jnp.sum(received.astype(jnp.float32), axis=0)

    shard = lax.axis_index("ctx")
    my_slots = shard * capacity + jnp.arange(capacity, dtype=jnp.int32)
    _, _, my_doc, my_pos = slot_table(my_slots, doc_len, doc_shard, doc_slot, capacity)
    heads_here = q_cols // HEAD_SIZE
    query_matrix = apply_rotary(
        summed[:, :q_cols].reshape(capacity, heads_here, HEAD_SIZE), my_pos
    ).astype(jnp.bfloat16)
    key_unrotated = lax.optimization_barrier(
        summed[:, q_cols : q_cols + HEAD_SIZE].astype(jnp.bfloat16)
    )
    value_matrix = summed[:, q_cols + HEAD_SIZE :].astype(jnp.bfloat16)
    key = apply_rotary(key_unrotated.astype(jnp.float32)[:, None, :], my_pos).astype(jnp.bfloat16)
    result = attend(
        query_matrix.reshape(capacity, 1, heads_here, HEAD_SIZE),
        key,
        value_matrix[:, None, :],
        my_doc,
        my_pos,
    )
    return result.reshape(capacity, heads_here * HEAD_SIZE)


def solution(mesh):
    return jax.shard_map(
        body,
        mesh=mesh,
        in_specs=(P(None, "ctx"), P("ctx", "tp"), P("ctx", "tp"), P("ctx", "tp"), P(), P(), P()),
        out_specs=P("ctx", "tp"),
        check_vma=False,
    )
```

time: 202 us -> 108 us (0.53)
  waiting for transfers between devices: 105 us -> 48.2 us
  local copies, waits for them, and re-layouts: 55.9 us -> 2.61 us
  blocking collectives: 0 us -> 29 us
  between operations: 13.8 us -> 0.22 us
  starting transfers between devices: 11.6 us -> 4.61 us
  matrix products: 8.44 us -> 15.1 us
  other arithmetic: 4.55 us -> 7.53 us
    reduce_scatter x1 -> x0, waiting for transfers between devices: 100 us -> none  [body(): lax.psum_scatter(jnp.where(filled[:, None] == 1, partial_rows, jnp.float3...]
    all_to_all x0 -> x1, waiting for transfers between devices: none -> 48.2 us  [body(): lax.all_to_all(slot_rows.reshape(shards, capacity, columns), 'ctx', 0, 0,...]
    scatter x4 -> x0, local copies, waits for them, and re-layouts: 32.2 us -> none  [the longest x1 8.06 us: slot_layout(): source = jnp.zeros((slot_total,), jnp.int32).at[target].set(token_ids)]
    all_gather x0 -> x1, blocking collectives: none -> 29 us  [body(): lax.all_gather(jnp.concatenate([wk, wv], axis=1), 'tp', axis=0, axis_inde...]
    gather x1 -> x0, local copies, waits for them, and re-layouts: 18.7 us -> none  [body(): picked = jnp.take(tokens, source, axis=0)]
    ppermute x3 -> x0, starting transfers between devices: 11.6 us -> none  [partner(): lax.ppermute(shard, axis, [(i, i ^ 1 << apart) for i in range(lax.axis_si...]
    dot_general x1 -> x3, matrix products: 7.81 us -> 14.5 us  [the longest x1 9.59 us: body(): jnp.dot(placement, term, preferred_element_type=jnp.float32)]
    ppermute x3 -> x0, waiting for transfers between devices: 4.77 us -> none  [partner(): lax.ppermute(shard, axis, [(i, i ^ 1 << apart) for i in range(lax.axis_si...]
  transfers between devices with their start and end apart: 4 -> 1, of which waited for: 3 -> 1; matrix products, arithmetic and copies ran while one was open for 9% -> 1% of each run, Pallas kernels for 0% -> 0%
where the time goes in v1:
time: 108 us; the launch traced here: 107 us
  waiting for transfers between devices  48.2 us (45%)
  blocking collectives  29 us (27%)
  matrix products  15.1 us (14%)
  other arithmetic  7.53 us (7%)
  starting transfers between devices  4.61 us (4%)
  local copies, waits for them, and re-layouts  2.61 us (2%)
    all_to_all x1, waiting for transfers between devices, body(): lax.all_to_all(slot_rows.reshape(shards, capacity, columns), 'ctx', 0, 0,...  48.2 us
    all_gather x1, blocking collectives, body(): lax.all_gather(jnp.concatenate([wk, wv], axis=1), 'tp', axis=0, axis_inde...  29 us
    dot_general x1, matrix products, body(): jnp.dot(placement, term, preferred_element_type=jnp.float32)  9.59 us
    all_to_all x1, starting transfers between devices, body(): lax.all_to_all(slot_rows.reshape(shards, capacity, columns), 'ctx', 0, 0,...  4.61 us
    dot_general x1, matrix products, body(): jnp.dot(tokens, wq, preferred_element_type=jnp.float32).astype(jnp.bfloat16)  3.63 us
    reduce_sum x1, other arithmetic, body(): summed = jnp.sum(received.astype(jnp.float32), axis=0)  2.37 us
  transfers between devices with their start and end apart: 1, of which 1 were waited for; matrix products, arithmetic and copies ran while one was open for 1% of the time, Pallas kernels for 0%

profile of v1, /device:TPU:1, one launch (start us, length us, event | category | flops | bytes accessed | tf_op | source)
XLA Modules:
  0.0 107.2 jit_solution(3175168633204208387)
XLA Ops:
  0.0 0.0 copy-start
  0.0 0.8 copy.22
  0.8 0.1 reduce-window.9
  0.9 0.1 reduce.2
  1.0 0.7 sub.71
  1.7 1.1 fusion.46
  2.8 1.0 fusion.17
  3.8 0.8 pad_maximum_fusion
  4.6 29.0 %all-gather = bf16[8192,32]{0,1:T(8,128)(2,1)S(1)} all-gather(bf16[1024,32]{0,1:T(8,128)(2,1)S(1)} %pad_maximum_fusion), channel_id=2, replica_groups={{0,1,2,3,4,5,6,7},{8,9,10,11,12,13,14,15},{16,17,18,19,20,21,22,23},{24..., dimensions={0}, use_global_device_ids=true | all-gather | bytes 589824 | tf_op jit(solution)/shard_map/all_gather | solution.py:75
  33.5 0.3 copy.32
  33.9 0.2 copy.23
  34.0 0.2 copy.24
  34.2 0.0 copy-done
  34.2 0.0 copy-start.4
  34.2 3.6 %convolution_convert_fusion.1 = bf16[2048,256]{0,1:T(8,128)(2,1)S(1)} fusion(bf16[2048,1024]{1,0:T(8,128)(2,1)} %param.7, bf16[1024,256]{1,0:T(8,128)(2,1)S(1)} %copy-done), kind=kOutput, calls=%fused_computation.8 | convolution fusion | flops 1074266112 | bytes 5767168 | tf_op jit(solution)/shard_map/dot_general | solution.py:88
  37.9 0.0 copy-done.4
  37.9 1.3 %fusion.8 = bf16[2048,256]{0,1:T(8,128)(2,1)S(1)} fusion(bf16[2048,1024]{1,0:T(8,128)(2,1)S(1)} %copy-done.4, bf16[1024,128]{0,1:T(8,128)(2,1)S(1)} %bitcast.65, bf16[1024,128]{0,1:T(8,128)(2,1)S(1)} %bitcast.64), kind=kOutput, calls=%fused_computation.9 | convolution fusion | flops 1075314688 | bytes 5767168 | tf_op jit(solution)/shard_map/dot_general | solution.py:89
  39.2 9.6 %fusion.5 = bf16[3072,512]{1,0:T(8,128)(2,1)} fusion(s32[3072]{0:T(1024)S(1)} %fusion.17, pred[3072]{0:T(1024)(128)(4,1)S(1)} %fusion.46, bf16[2048,256]{0,1:T(8,128)(2,1)S(1)} %fusion.8, bf16[2048,256]{0,1:T(8,128)(2,1)S(1)} %convolution_convert_fusion.1), kind=kOutput, calls=%fused_computation.6 | convolution fusion | flops 6460801024 | bytes 5258240 | tf_op jit(solution)/shard_map/dot_general | solution.py:93
  48.8 0.0 copy-start.1
  48.8 0.0 copy-start.2
  48.8 0.0 copy-start.3
  48.8 4.6 %all-to-all-start = ((bf16[16,192,512]{2,1,0:T(8,128)(2,1)}), bf16[16,192,512]{2,1,0:T(8,128)(2,1)}, u32[]{:S(2)}, u32[]{:S(2)}) async-start(bf16[16,192,512]{2,1,0:T(8,128)(2,1)} %bitcast.60), calls=%async_computation | async-start | bytes 6291456 | tf_op jit(solution)/shard_map/all_to_all | solution.py:95
  53.4 0.0 copy-done.1
  53.4 0.0 copy-done.2
  53.4 0.0 copy-done.3
  53.4 0.1 select_reduce_fusion
  53.6 0.1 fusion.59
  53.7 0.1 compare_and_fusion
  53.8 0.4 multiply_cosine_fusion
  54.2 48.2 %all-to-all-done = bf16[16,192,512]{2,1,0:T(8,128)(2,1)} async-done(((bf16[16,192,512]{2,1,0:T(8,128)(2,1)}), bf16[16,192,512]{2,1,0:T(8,128)(2,1)}, u32[]{:S(2)}, u32[]{:S(2)}) %all-to-all-start) | async-done | bytes 3145760 | tf_op jit(solution)/shard_map/all_to_all | solution.py:95
  102.4 2.4 %convert_reduce_fusion = f32[192,512]{1,0:T(8,128)S(1)} fusion(bf16[16,192,512]{2,1,0:T(8,128)(2,1)} %all-to-all-done), kind=kLoop, calls=%fused_computation.5 | loop fusion | flops 3047424 | bytes 3538944 | tf_op jit(solution)/shard_map/reduce_sum | solution.py:98
  104.8 0.1 reshape.306
  104.9 0.3 fusion.60
  105.2 0.5 fusion.45
  105.7 0.1 subtract_convert_fusion
  105.8 0.3 fusion.61
  106.1 0.1 fusion.23
  106.2 0.3 fusion.15
  106.5 0.1 copy.28
  106.6 0.7 copy.39
  (10 shorter events, 0.1 us)
Async XLA Ops:
  0.0 34.2 %copy-start = (bf16[1024,256]{1,0:T(8,128)(2,1)S(1)}, bf16[1024,256]{1,0:T(8,128)(2,1)}, u32[]{:S(2)}) copy-start(bf16[1024,256]{1,0:T(8,128)(2,1)} %param.8) | copy-start | bytes 1572868
  34.2 3.7 %copy-start.4 = (bf16[2048,1024]{1,0:T(8,128)(2,1)S(1)}, bf16[2048,1024]{1,0:T(8,128)(2,1)}, u32[]{:S(2)}) copy-start(bf16[2048,1024]{1,0:T(8,128)(2,1)} %param.7) | copy-start | bytes 12582916
  48.8 4.7 %copy-start.1 = (s32[64]{0:T(128)S(1)}, s32[64]{0:T(128)}, u32[]{:S(2)}) copy-start(s32[64]{0:T(128)} %param.11) | copy-start | bytes 772
  48.8 4.7 %copy-start.2 = (s32[64]{0:T(128)S(1)}, s32[64]{0:T(128)}, u32[]{:S(2)}) copy-start(s32[64]{0:T(128)} %param.13) | copy-start | bytes 772
  48.8 4.7 %copy-start.3 = (s32[64]{0:T(128)S(1)}, s32[64]{0:T(128)}, u32[]{:S(2)}) copy-start(s32[64]{0:T(128)} %param.12) | copy-start | bytes 772
  48.8 53.6 %all-to-all-start = ((bf16[16,192,512]{2,1,0:T(8,128)(2,1)}), bf16[16,192,512]{2,1,0:T(8,128)(2,1)}, u32[]{:S(2)}, u32[]{:S(2)}) async-start(bf16[16,192,512]{2,1,0:T(8,128)(2,1)} %bitcast.60), calls=%async_computation | async-start | bytes 6291456 | tf_op jit(solution)/shard_map/all_to_all | solution.py:95

commit v2 on v1

--- a/solution.py
+++ b/solution.py
@@ -72,12 +72,6 @@
         list(range(g * members, (g + 1) * members))
         for g in range(lax.axis_size("tp") // members)
     ]
-    pieces = lax.all_gather(
-        jnp.concatenate([wk, wv], axis=1), "tp", axis=0, axis_index_groups=groups
-    )
-    width = pieces.shape[1]
-    key_weights = jnp.transpose(pieces[:, :, :key_value_columns], (1, 0, 2)).reshape(width, HEAD_SIZE)
-    value_weights = jnp.transpose(pieces[:, :, key_value_columns:], (1, 0, 2)).reshape(width, HEAD_SIZE)
 
     source, filled, _, _ = slot_table(
         jnp.arange(slot_total, dtype=jnp.int32), doc_len, doc_shard, doc_slot, capacity
@@ -85,17 +79,20 @@
     token_ids = jnp.arange(total_tokens, dtype=jnp.int32)
     placement = ((source[:, None] == token_ids[None, :]) & filled[:, None]).astype(jnp.bfloat16)
 
-    query_term = jnp.dot(tokens, wq, preferred_element_type=jnp.float32).astype(jnp.bfloat16)
-    kv_term = jnp.dot(
-        tokens, jnp.concatenate([key_weights, value_weights], axis=1), preferred_element_type=jnp.float32
-    ).astype(jnp.bfloat16)
-    term = jnp.concatenate([query_term, kv_term], axis=1)
+    joined = jnp.concatenate([wq, wk, wv], axis=1)
+    term = jnp.dot(tokens, joined, preferred_element_type=jnp.float32).astype(jnp.bfloat16)
     slot_rows = jnp.dot(placement, term, preferred_element_type=jnp.float32).astype(jnp.bfloat16)
     columns = slot_rows.shape[1]
     received = lax.all_to_all(
         slot_rows.reshape(shards, capacity, columns), "ctx", 0, 0, tiled=False
     )
     summed = jnp.sum(received.astype(jnp.float32), axis=0)
+
+    pieces = lax.all_gather(
+        summed[:, q_cols:].astype(jnp.bfloat16), "tp", axis=0, axis_index_groups=groups
+    )
+    key_unrotated = jnp.transpose(pieces[:, :, :key_value_columns], (1, 0, 2)).reshape(capacity, HEAD_SIZE)
+    value_matrix = jnp.transpose(pieces[:, :, key_value_columns:], (1, 0, 2)).reshape(capacity, HEAD_SIZE)
 
     shard = lax.axis_index("ctx")
     my_slots = shard * capacity + jnp.arange(capacity, dtype=jnp.int32)
@@ -104,10 +101,6 @@
     query_matrix = apply_rotary(
         summed[:, :q_cols].reshape(capacity, heads_here, HEAD_SIZE), my_pos
     ).astype(jnp.bfloat16)
-    key_unrotated = lax.optimization_barrier(
-        summed[:, q_cols : q_cols + HEAD_SIZE].astype(jnp.bfloat16)
-    )
-    value_matrix = summed[:, q_cols + HEAD_SIZE :].astype(jnp.bfloat16)
     key = apply_rotary(key_unrotated.astype(jnp.float32)[:, None, :], my_pos).astype(jnp.bfloat16)
     result = attend(
         query_matrix.reshape(capacity, 1, heads_here, HEAD_SIZE),

time: 108 us -> 87.1 us (0.81)
  waiting for transfers between devices: 48.2 us -> 23.8 us
  local copies, waits for them, and re-layouts: 2.61 us -> 10.1 us
  starting transfers between devices: 4.61 us -> 7.7 us
  other arithmetic: 7.53 us -> 4.75 us
  blocking collectives: 29 us -> 26.5 us
  matrix products: 15.1 us -> 13.6 us
    all_to_all x1, waiting for transfers between devices: 48.2 us -> 23.8 us  [body(): lax.all_to_all(slot_rows.reshape(shards, capacity, columns), 'ctx', 0, 0,...]
    reshape x1 -> x2, local copies, waits for them, and re-layouts: 0.1 us -> 6.23 us  [body(): slot_rows.reshape(shards, capacity, columns)]
    all_to_all x1, starting transfers between devices: 4.61 us -> 7.7 us  [body(): lax.all_to_all(slot_rows.reshape(shards, capacity, columns), 'ctx', 0, 0,...]
    all_gather x1, blocking collectives: 29 us -> 26.5 us  [body(): lax.all_gather(summed[:, q_cols:].astype(jnp.bfloat16), 'tp', axis=0, axi...]
    reduce_sum x1, other arithmetic: 2.37 us -> 0.4 us  [body(): summed = jnp.sum(received.astype(jnp.float32), axis=0)]
    unnamed x12 -> x14, local copies, waits for them, and re-layouts: 0.97 us -> 2.94 us
    dot_general x2 -> x1, matrix products: 4.92 us -> 4.37 us  [body(): jnp.dot(tokens, joined, preferred_element_type=jnp.float32)]
where the time goes in v2:
time: 87.1 us; the launch traced here: 86.6 us
  blocking collectives  26.5 us (30%)
  waiting for transfers between devices  23.8 us (27%)
  matrix products  13.6 us (16%)
  local copies, waits for them, and re-layouts  10.1 us (12%)
  starting transfers between devices  7.7 us (9%)
  other arithmetic  4.75 us (5%)
    all_gather x1, blocking collectives, body(): lax.all_gather(summed[:, q_cols:].astype(jnp.bfloat16), 'tp', axis=0, axi...  26.5 us
    all_to_all x1, waiting for transfers between devices, body(): lax.all_to_all(slot_rows.reshape(shards, capacity, columns), 'ctx', 0, 0,...  23.8 us
    dot_general x1, matrix products, body(): jnp.dot(placement, term, preferred_element_type=jnp.float32)  8.6 us
    all_to_all x1, starting transfers between devices, body(): lax.all_to_all(slot_rows.reshape(shards, capacity, columns), 'ctx', 0, 0,...  7.7 us
    reshape x2, local copies, waits for them, and re-layouts, body(): slot_rows.reshape(shards, capacity, columns)  6.23 us
    dot_general x1, matrix products, body(): jnp.dot(tokens, joined, preferred_element_type=jnp.float32)  4.37 us
    unnamed x14, local copies, waits for them, and re-layouts  2.94 us
  transfers between devices with their start and end apart: 1, of which 1 were waited for; matrix products, arithmetic and copies ran while one was open for 1% of the time, Pallas kernels for 0%

profile of v2, /device:TPU:1, one launch (start us, length us, event | category | flops | bytes accessed | tf_op | source)
XLA Modules:
  0.0 86.6 jit_solution(4568909548194425633)
XLA Ops:
  0.0 0.7 copy.35
  0.8 0.1 reduce-window.9
  0.9 0.1 reduce.2
  1.0 0.7 sub.71
  1.6 1.1 %fusion.49 = pred[3072]{0:T(1024)(128)(4,1)S(1)} fusion(s32[64]{0:T(128)} %param.11, s32[64]{0:T(128)} %param.13, s32[3072]{0:T(1024)S(1)} %get-tuple-element.21, s32[64]{0:T(128)} %param.12, s32[3072]{0:T(1024)S(1)} %get-tuple-element.22), kind=kLoop, calls=%fused_computation.63 | loop fusion | flops 1373184 | bytes 28416 | tf_op jit(solution)/shard_map/reduce_or | solution.py:21
  2.7 1.0 %fusion.13 = s32[3072]{0:T(1024)S(1)} fusion(s32[64]{0:T(128)S(1)} %sub.71, s32[64]{0:T(128)} %param.13, s32[3072]{0:T(1024)S(1)} %get-tuple-element.21, s32[64]{0:T(128)} %param.11, s32[64]{0:T(128)} %param.12, s32[3072]{0:T(1024)S(1)} %get-tuple-element.22), kind=kLoop, calls=%fused_computation.18 | loop fusion | flops 1766400 | bytes 37888 | tf_op jit(solution)/shard_map/reduce_sum | solution.py:23
  3.7 0.9 %copy.37 = bf16[1024,16]{1,0:T(8,128)(2,1)S(1)} copy(bf16[1024,16]{0,1:T(8,128)(2,1)} %param.10) | data formatting | bytes 65536 | tf_op args[3]
  4.6 0.9 %copy.36 = bf16[1024,16]{1,0:T(8,128)(2,1)S(1)} copy(bf16[1024,16]{0,1:T(8,128)(2,1)} %param.9) | data formatting | bytes 65536 | tf_op args[2]
  5.6 4.4 %convolution_convert_fusion.clone.5 = bf16[288,2048]{1,0:T(8,128)(2,1)S(1)} fusion(bf16[2048,1024]{1,0:T(8,128)(2,1)} %param.7, bf16[1024,16]{1,0:T(8,128)(2,1)S(1)} %copy.37, bf16[1024,16]{1,0:T(8,128)(2,1)S(1)} %copy.36, bf16[1024,256]{1,0:T(8,128)(2,1)} %param.8), kind=kOutput, calls=%fused_computation.7.clone.clone.clone.2 | convolution fusion | flops 1210318848 | bytes 5963776 | tf_op jit(solution)/shard_map/dot_general | solution.py:83
  10.0 8.6 %fusion.5 = bf16[3072,288]{0,1:T(8,128)(2,1)} fusion(s32[3072]{0:T(1024)S(1)} %fusion.13, pred[3072]{0:T(1024)(128)(4,1)S(1)} %fusion.49, bf16[288,2048]{1,0:T(8,128)(2,1)S(1)} %convolution_convert_fusion.clone.5), kind=kOutput, calls=%fused_computation.6 | convolution fusion | flops 3637346304 | bytes 2964480 | tf_op jit(solution)/shard_map/dot_general | solution.py:84
  18.6 4.0 %reshape.312 = bf16[16,192,288]{1,0,2:T(8,128)(2,1)S(1)} reshape(bf16[3072,288]{0,1:T(8,128)(2,1)} %fusion.5) | data formatting | bytes 3538944 | tf_op jit(solution)/shard_map/reshape | solution.py:87
  22.6 2.2 %copy.38 = bf16[16,192,288]{1,2,0:T(8,128)(2,1)} copy(bf16[16,192,288]{1,0,2:T(8,128)(2,1)S(1)} %reshape.312) | data formatting | bytes 3538944 | tf_op jit(solution)/shard_map/reshape | solution.py:87
  24.8 0.0 copy-start
  24.8 0.0 copy-start.1
  24.8 0.0 copy-start.2
  24.8 7.7 %all-to-all-start = ((bf16[16,192,288]{1,2,0:T(8,128)(2,1)}), bf16[16,192,288]{1,2,0:T(8,128)(2,1)S(1)}, u32[]{:S(2)}, u32[]{:S(2)}) async-start(bf16[16,192,288]{1,2,0:T(8,128)(2,1)} %copy.38), calls=%async_computation | async-start | bytes 4718592 | tf_op jit(solution)/shard_map/all_to_all | solution.py:86
  32.5 0.0 copy-done
  32.6 0.0 copy-done.1
  32.6 0.0 copy-done.2
  32.6 0.1 select_reduce_fusion
  32.7 0.1 fusion.63
  32.8 0.1 compare_and_fusion
  33.0 0.4 multiply_cosine_fusion
  33.4 23.8 %all-to-all-done = bf16[16,192,288]{1,2,0:T(8,128)(2,1)S(1)} async-done(((bf16[16,192,288]{1,2,0:T(8,128)(2,1)}), bf16[16,192,288]{1,2,0:T(8,128)(2,1)S(1)}, u32[]{:S(2)}, u32[]{:S(2)}) %all-to-all-start) | async-done | bytes 1769504 | tf_op jit(solution)/shard_map/all_to_all | solution.py:86
  57.2 0.4 convert_reduce_fusion
  57.7 26.5 %all-gather.1 = bf16[8,192,32]{1,2,0:T(8,128)(2,1)S(1)} all-gather(bf16[1,192,32]{1,2,0:T(8,128)(2,1)S(1)} %fusion.54), channel_id=2, replica_groups={{0,1,2,3,4,5,6,7},{8,9,10,11,12,13,14,15},{16,17,18,19,20,21,22,23},{24..., dimensions={0}, use_global_device_ids=true | all-gather | bytes 110592 | tf_op jit(solution)/shard_map/all_gather | solution.py:91
  84.2 0.1 copy.56
  84.3 0.1 copy.55
  84.5 0.1 copy.54
  84.6 0.1 copy.53
  84.7 0.4 fusion.46
  85.1 0.1 subtract_convert_fusion
  85.2 0.3 fusion.66
  85.5 0.1 fusion.26
  85.6 0.3 fusion.11
  85.9 0.1 copy.46
  86.0 0.7 copy.59
  (10 shorter events, 0.1 us)
Async XLA Ops:
  24.8 7.7 %copy-start = (s32[64]{0:T(128)S(1)}, s32[64]{0:T(128)}, u32[]{:S(2)}) copy-start(s32[64]{0:T(128)} %param.11) | copy-start | bytes 772
  24.8 7.8 %copy-start.1 = (s32[64]{0:T(128)S(1)}, s32[64]{0:T(128)}, u32[]{:S(2)}) copy-start(s32[64]{0:T(128)} %param.13) | copy-start | bytes 772
  24.8 7.8 %copy-start.2 = (s32[64]{0:T(128)S(1)}, s32[64]{0:T(128)}, u32[]{:S(2)}) copy-start(s32[64]{0:T(128)} %param.12) | copy-start | bytes 772
  24.8 32.4 %all-to-all-start = ((bf16[16,192,288]{1,2,0:T(8,128)(2,1)}), bf16[16,192,288]{1,2,0:T(8,128)(2,1)S(1)}, u32[]{:S(2)}, u32[]{:S(2)}) async-start(bf16[16,192,288]{1,2,0:T(8,128)(2,1)} %copy.38), calls=%async_computation | async-start | bytes 4718592 | tf_op jit(solution)/shard_map/all_to_all | solution.py:86

commit v3 on v2

--- a/solution.py
+++ b/solution.py
@@ -81,12 +81,14 @@
 
     joined = jnp.concatenate([wq, wk, wv], axis=1)
     term = jnp.dot(tokens, joined, preferred_element_type=jnp.float32).astype(jnp.bfloat16)
-    slot_rows = jnp.dot(placement, term, preferred_element_type=jnp.float32).astype(jnp.bfloat16)
-    columns = slot_rows.shape[1]
-    received = lax.all_to_all(
-        slot_rows.reshape(shards, capacity, columns), "ctx", 0, 0, tiled=False
-    )
-    summed = jnp.sum(received.astype(jnp.float32), axis=0)
+    slot_rows = jnp.einsum(
+        "jf,csj->cfs",
+        term,
+        placement.reshape(shards, capacity, total_tokens),
+        preferred_element_type=jnp.float32,
+    ).astype(jnp.bfloat16)
+    received = lax.all_to_all(slot_rows, "ctx", 0, 0, tiled=False)
+    summed = jnp.transpose(jnp.sum(received.astype(jnp.float32), axis=0))
 
     pieces = lax.all_gather(
         summed[:, q_cols:].astype(jnp.bfloat16), "tp", axis=0, axis_index_groups=groups

time: 87.1 us -> 81.2 us (0.932)
  local copies, waits for them, and re-layouts: 10.1 us -> 4.23 us
    reshape x2 -> x1, local copies, waits for them, and re-layouts: 6.23 us -> 0.1 us  [body(): summed[:, :q_cols].reshape(capacity, heads_here, HEAD_SIZE)]
    unnamed x14 -> x11, local copies, waits for them, and re-layouts: 2.94 us -> 2.75 us
where the time goes in v3:
time: 81.2 us; the launch traced here: 80.8 us
  blocking collectives  26.5 us (33%)
  waiting for transfers between devices  23.8 us (29%)
  matrix products  13.6 us (17%)
  starting transfers between devices  7.71 us (9%)
  other arithmetic  4.73 us (6%)
  local copies, waits for them, and re-layouts  4.23 us (5%)
    all_gather x1, blocking collectives, body(): lax.all_gather(summed[:, q_cols:].astype(jnp.bfloat16), 'tp', axis=0, axi...  26.5 us
    all_to_all x1, waiting for transfers between devices, body(): received = lax.all_to_all(slot_rows, 'ctx', 0, 0, tiled=False)  23.8 us
    dot_general x1, matrix products, body(): jnp.einsum('jf,csj->cfs', term, placement.reshape(shards, capacity, total...  8.64 us
    all_to_all x1, starting transfers between devices, body(): received = lax.all_to_all(slot_rows, 'ctx', 0, 0, tiled=False)  7.71 us
    dot_general x1, matrix products, body(): jnp.dot(tokens, joined, preferred_element_type=jnp.float32)  4.38 us
    unnamed x11, local copies, waits for them, and re-layouts  2.75 us
  transfers between devices with their start and end apart: 1, of which 1 were waited for; matrix products, arithmetic and copies ran while one was open for 1% of the time, Pallas kernels for 0%

profile of v3, /device:TPU:1, one launch (start us, length us, event | category | flops | bytes accessed | tf_op | source)
XLA Modules:
  0.0 80.8 jit_solution(8240606565759003256)
XLA Ops:
  0.0 0.7 copy.34
  0.8 0.1 reduce-window.9
  0.9 0.1 reduce.2
  1.0 0.7 sub.71
  1.6 1.1 %fusion.46 = pred[3072]{0:T(1024)(128)(4,1)S(1)} fusion(s32[64]{0:T(128)} %param.11, s32[64]{0:T(128)} %param.13, s32[3072]{0:T(1024)S(1)} %get-tuple-element.21, s32[64]{0:T(128)} %param.12, s32[3072]{0:T(1024)S(1)} %get-tuple-element.22), kind=kLoop, calls=%fused_computation.65 | loop fusion | flops 1373184 | bytes 28416 | tf_op jit(solution)/shard_map/reduce_or | solution.py:21
  2.7 1.0 %fusion.13 = s32[3072]{0:T(1024)S(1)} fusion(s32[64]{0:T(128)S(1)} %sub.71, s32[64]{0:T(128)} %param.13, s32[3072]{0:T(1024)S(1)} %get-tuple-element.21, s32[64]{0:T(128)} %param.11, s32[64]{0:T(128)} %param.12, s32[3072]{0:T(1024)S(1)} %get-tuple-element.22), kind=kLoop, calls=%fused_computation.19 | loop fusion | flops 1766400 | bytes 37888 | tf_op jit(solution)/shard_map/reduce_sum | solution.py:23
  3.7 0.1 eq.66
  3.8 0.1 and.67
  3.9 0.9 %copy.36 = bf16[1024,16]{1,0:T(8,128)(2,1)S(1)} copy(bf16[1024,16]{0,1:T(8,128)(2,1)} %param.10) | data formatting | bytes 65536 | tf_op args[3]
  4.8 1.0 %copy.35 = bf16[1024,16]{1,0:T(8,128)(2,1)S(1)} copy(bf16[1024,16]{0,1:T(8,128)(2,1)} %param.9) | data formatting | bytes 65536 | tf_op args[2]
  5.8 4.4 %fusion.5.clone.5 = bf16[288,2048,1]{1,0,2:T(8,128)(2,1)S(1)} fusion(bf16[2048,1024]{1,0:T(8,128)(2,1)} %param.7, bf16[1024,16]{1,0:T(8,128)(2,1)S(1)} %copy.36, bf16[1024,16]{1,0:T(8,128)(2,1)S(1)} %copy.35, bf16[1024,256]{1,0:T(8,128)(2,1)} %param.8), kind=kOutput, calls=%fused_computation.7.clone.clone.clone.2 | convolution fusion | flops 1210318848 | bytes 5963776 | tf_op jit(solution)/shard_map/dot_general | solution.py:83
  10.2 8.6 %convert_bitcast_fusion = bf16[16,288,192]{1,2,0:T(8,128)(2,1)} fusion(s32[16,192]{1,0:T(8,128)S(1)} %eq.66, pred[16,192]{1,0:T(8,128)(4,1)S(1)} %and.67, bf16[288,2048,1]{1,0,2:T(8,128)(2,1)S(1)} %fusion.5.clone.5), kind=kOutput, calls=%fused_computation.8 | convolution fusion | flops 3637346304 | bytes 2964480 | tf_op jit(solution)/shard_map/jf,csj->cfs/dot_general | solution.py:84
  18.8 0.0 copy-start
  18.8 0.0 copy-start.1
  18.8 0.0 copy-start.2
  18.8 7.7 %all-to-all-start = ((bf16[16,288,192]{1,2,0:T(8,128)(2,1)}), bf16[16,288,192]{1,2,0:T(8,128)(2,1)S(1)}, u32[]{:S(2)}, u32[]{:S(2)}) async-start(bf16[16,288,192]{1,2,0:T(8,128)(2,1)} %convert_bitcast_fusion), calls=%async_computation | async-start | bytes 4718592 | tf_op jit(solution)/shard_map/all_to_all | solution.py:90
  26.6 0.0 copy-done
  26.6 0.0 copy-done.1
  26.6 0.0 copy-done.2
  26.6 0.1 select_reduce_fusion
  26.7 0.1 fusion.59
  26.9 0.1 compare_and_fusion
  27.0 0.4 multiply_cosine_fusion
  27.4 23.8 %all-to-all-done = bf16[16,288,192]{1,2,0:T(8,128)(2,1)S(1)} async-done(((bf16[16,288,192]{1,2,0:T(8,128)(2,1)}), bf16[16,288,192]{1,2,0:T(8,128)(2,1)S(1)}, u32[]{:S(2)}, u32[]{:S(2)}) %all-to-all-start) | async-done | bytes 1769504 | tf_op jit(solution)/shard_map/all_to_all | solution.py:90
  51.2 0.4 convert_reduce_fusion
  51.7 0.1 copy.37
  51.7 26.5 %all-gather.1 = bf16[8,192,32]{1,2,0:T(8,128)(2,1)S(1)} all-gather(bf16[1,192,32]{1,2,0:T(8,128)(2,1)S(1)} %bitcast.72), channel_id=2, replica_groups={{0,1,2,3,4,5,6,7},{8,9,10,11,12,13,14,15},{16,17,18,19,20,21,22,23},{24..., dimensions={0}, use_global_device_ids=true | all-gather | bytes 110592 | tf_op jit(solution)/shard_map/all_gather | solution.py:93
  78.2 0.1 reshape.324
  78.3 0.3 fusion.60
  78.6 0.1 copy.49
  78.7 0.1 copy.48
  78.8 0.4 fusion.43
  79.3 0.1 subtract_convert_fusion
  79.3 0.3 fusion.62
  79.6 0.1 fusion.23
  79.7 0.3 fusion.11
  80.0 0.1 copy.44
  80.1 0.7 copy.58
  (9 shorter events, 0.1 us)
Async XLA Ops:
  18.8 7.8 %copy-start = (s32[64]{0:T(128)S(1)}, s32[64]{0:T(128)}, u32[]{:S(2)}) copy-start(s32[64]{0:T(128)} %param.11) | copy-start | bytes 772
  18.8 7.8 %copy-start.1 = (s32[64]{0:T(128)S(1)}, s32[64]{0:T(128)}, u32[]{:S(2)}) copy-start(s32[64]{0:T(128)} %param.13) | copy-start | bytes 772
  18.8 7.8 %copy-start.2 = (s32[64]{0:T(128)S(1)}, s32[64]{0:T(128)}, u32[]{:S(2)}) copy-start(s32[64]{0:T(128)} %param.12) | copy-start | bytes 772
  18.8 32.4 %all-to-all-start = ((bf16[16,288,192]{1,2,0:T(8,128)(2,1)}), bf16[16,288,192]{1,2,0:T(8,128)(2,1)S(1)}, u32[]{:S(2)}, u32[]{:S(2)}) async-start(bf16[16,288,192]{1,2,0:T(8,128)(2,1)} %convert_bitcast_fusion), calls=%async_computation | async-start | bytes 4718592 | tf_op jit(solution)/shard_map/all_to_all | solution.py:90

commit v4 on v3

--- a/solution.py
+++ b/solution.py
@@ -87,12 +87,13 @@
         placement.reshape(shards, capacity, total_tokens),
         preferred_element_type=jnp.float32,
     ).astype(jnp.bfloat16)
-    received = lax.all_to_all(slot_rows, "ctx", 0, 0, tiled=False)
-    summed = jnp.transpose(jnp.sum(received.astype(jnp.float32), axis=0))
-
+    kv_received = lax.all_to_all(slot_rows[:, q_cols:], "ctx", 0, 0, tiled=False)
+    kv_summed = lax.optimization_barrier(jnp.sum(kv_received.astype(jnp.float32), axis=0))
     pieces = lax.all_gather(
-        summed[:, q_cols:].astype(jnp.bfloat16), "tp", axis=0, axis_index_groups=groups
+        jnp.transpose(kv_summed).astype(jnp.bfloat16), "tp", axis=0, axis_index_groups=groups
     )
+    q_received = lax.all_to_all(slot_rows[:, :q_cols], "ctx", 0, 0, tiled=False)
+    q_summed = jnp.transpose(jnp.sum(q_received.astype(jnp.float32), axis=0))
     key_unrotated = jnp.transpose(pieces[:, :, :key_value_columns], (1, 0, 2)).reshape(capacity, HEAD_SIZE)
     value_matrix = jnp.transpose(pieces[:, :, key_value_columns:], (1, 0, 2)).reshape(capacity, HEAD_SIZE)
 
@@ -101,7 +102,7 @@
     _, _, my_doc, my_pos = slot_table(my_slots, doc_len, doc_shard, doc_slot, capacity)
     heads_here = q_cols // HEAD_SIZE
     query_matrix = apply_rotary(
-        summed[:, :q_cols].reshape(capacity, heads_here, HEAD_SIZE), my_pos
+        q_summed.reshape(capacity, heads_here, HEAD_SIZE), my_pos
     ).astype(jnp.bfloat16)
     key = apply_rotary(key_unrotated.astype(jnp.float32)[:, None, :], my_pos).astype(jnp.bfloat16)
     result = attend(

time: 81.2 us -> 70 us (0.86)
  waiting for transfers between devices: 23.8 us -> 6.01 us
  starting transfers between devices: 7.71 us -> 11.3 us
  local copies, waits for them, and re-layouts: 4.23 us -> 6.72 us
  blocking collectives: 26.5 us -> 27.9 us
    all_to_all x1 -> x2, waiting for transfers between devices: 23.8 us -> 6.01 us  [the longest x1 6.01 us: body(): lax.all_to_all(slot_rows[:, q_cols:], 'ctx', 0, 0, tiled=False)]
    all_to_all x1 -> x2, starting transfers between devices: 7.71 us -> 11.3 us  [the longest x1 7.57 us: body(): lax.all_to_all(slot_rows[:, q_cols:], 'ctx', 0, 0, tiled=False)]
    slice x3, local copies, waits for them, and re-layouts: 0.09 us -> 2.43 us  [the longest x1 1.27 us: body(): q_received = lax.all_to_all(slot_rows[:, :q_cols], 'ctx', 0, 0, tiled=False)]
    all_gather x1, blocking collectives: 26.5 us -> 27.9 us  [body(): lax.all_gather(jnp.transpose(kv_summed).astype(jnp.bfloat16), 'tp', axis=...]
    unnamed x11 -> x12, local copies, waits for them, and re-layouts: 2.75 us -> 2.83 us
  transfers between devices with their start and end apart: 1 -> 2, of which waited for: 1 -> 1; matrix products, arithmetic and copies ran while one was open for 1% -> 4% of each run, Pallas kernels for 0% -> 0%
where the time goes in v4:
time: 70 us; the launch traced here: 69.6 us
  blocking collectives  27.9 us (40%)
  matrix products  12.8 us (18%)
  starting transfers between devices  11.3 us (16%)
  local copies, waits for them, and re-layouts  6.72 us (10%)
  waiting for transfers between devices  6.01 us (9%)
  other arithmetic  4.62 us (7%)
    all_gather x1, blocking collectives, body(): lax.all_gather(jnp.transpose(kv_summed).astype(jnp.bfloat16), 'tp', axis=...  27.9 us
    dot_general x1, matrix products, body(): jnp.einsum('jf,csj->cfs', term, placement.reshape(shards, capacity, total...  7.84 us
    all_to_all x1, starting transfers between devices, body(): lax.all_to_all(slot_rows[:, q_cols:], 'ctx', 0, 0, tiled=False)  7.57 us
    all_to_all x1, waiting for transfers between devices, body(): lax.all_to_all(slot_rows[:, q_cols:], 'ctx', 0, 0, tiled=False)  6.01 us
    dot_general x1, matrix products, body(): jnp.dot(tokens, joined, preferred_element_type=jnp.float32)  4.37 us
    all_to_all x1, starting transfers between devices, body(): q_received = lax.all_to_all(slot_rows[:, :q_cols], 'ctx', 0, 0, tiled=False)  3.71 us
    unnamed x12, local copies, waits for them, and re-layouts  2.83 us
  transfers between devices with their start and end apart: 2, of which 1 were waited for; matrix products, arithmetic and copies ran while one was open for 4% of the time, Pallas kernels for 0%

profile of v4, /device:TPU:1, one launch (start us, length us, event | category | flops | bytes accessed | tf_op | source)
XLA Modules:
  0.0 69.6 jit_solution(12871037447029811625)
XLA Ops:
  0.0 0.7 %copy.35 = s32[64,1]{1,0:T(8,128)S(1)} copy(s32[64,1]{0,1:T(1,128)} %bitcast.76) | data formatting | bytes 512 | tf_op jit(solution)/shard_map/reshape.295
  0.8 0.1 reduce-window.9
  0.9 0.1 reduce.2
  1.0 0.7 sub.71
  1.6 1.1 %fusion.46 = pred[3072]{0:T(1024)(128)(4,1)S(1)} fusion(s32[64]{0:T(128)} %param.11, s32[64]{0:T(128)} %param.13, s32[3072]{0:T(1024)S(1)} %get-tuple-element.21, s32[64]{0:T(128)} %param.12, s32[3072]{0:T(1024)S(1)} %get-tuple-element.22), kind=kLoop, calls=%fused_computation.66 | loop fusion | flops 1373184 | bytes 28416 | tf_op jit(solution)/shard_map/reduce_or | solution.py:21
  2.7 1.0 %fusion.13 = s32[3072]{0:T(1024)S(1)} fusion(s32[64]{0:T(128)S(1)} %sub.71, s32[64]{0:T(128)} %param.13, s32[3072]{0:T(1024)S(1)} %get-tuple-element.21, s32[64]{0:T(128)} %param.11, s32[64]{0:T(128)} %param.12, s32[3072]{0:T(1024)S(1)} %get-tuple-element.22), kind=kLoop, calls=%fused_computation.19 | loop fusion | flops 1766400 | bytes 37888 | tf_op jit(solution)/shard_map/reduce_sum | solution.py:23
  3.7 0.1 eq.66
  3.8 0.1 and.67
  3.9 0.9 %copy.37 = bf16[1024,16]{1,0:T(8,128)(2,1)S(1)} copy(bf16[1024,16]{0,1:T(8,128)(2,1)} %param.10) | data formatting | bytes 65536 | tf_op args[3]
  4.8 0.9 %copy.36 = bf16[1024,16]{1,0:T(8,128)(2,1)S(1)} copy(bf16[1024,16]{0,1:T(8,128)(2,1)} %param.9) | data formatting | bytes 65536 | tf_op args[2]
  5.7 4.4 %fusion.5.clone.5 = bf16[288,2048,1]{1,0,2:T(8,128)(2,1)S(1)} fusion(bf16[2048,1024]{1,0:T(8,128)(2,1)} %param.7, bf16[1024,16]{1,0:T(8,128)(2,1)S(1)} %copy.37, bf16[1024,16]{1,0:T(8,128)(2,1)S(1)} %copy.36, bf16[1024,256]{1,0:T(8,128)(2,1)} %param.8), kind=kOutput, calls=%fused_computation.7.clone.clone.clone.2 | convolution fusion | flops 1210318848 | bytes 5963776 | tf_op jit(solution)/shard_map/dot_general | solution.py:83
  10.1 7.8 %convert_bitcast_fusion = bf16[16,288,192]{1,2,0:T(8,128)(2,1)S(1)} fusion(s32[16,192]{1,0:T(8,128)S(1)} %eq.66, pred[16,192]{1,0:T(8,128)(4,1)S(1)} %and.67, bf16[288,2048,1]{1,0,2:T(8,128)(2,1)S(1)} %fusion.5.clone.5), kind=kOutput, calls=%fused_computation.8 | convolution fusion | flops 3637346304 | bytes 2964480 | tf_op jit(solution)/shard_map/jf,csj->cfs/dot_general | solution.py:84
  18.0 0.1 slice.32
  18.1 0.0 copy-start
  18.1 0.0 copy-start.1
  18.1 0.0 copy-start.2
  18.1 1.0 %copy.38 = bf16[16,32,192]{2,1,0:T(8,128)(2,1)} copy(bf16[16,32,192]{1,2,0:T(8,128)(2,1)S(1)} %slice.32) | data formatting | bytes 393216 | tf_op jit(solution)/shard_map/slice | solution.py:90
  19.2 7.6 %all-to-all-start = ((bf16[16,32,192]{2,1,0:T(8,128)(2,1)}), bf16[16,32,192]{2,1,0:T(8,128)(2,1)S(1)}, u32[]{:S(2)}, u32[]{:S(2)}) async-start(bf16[16,32,192]{2,1,0:T(8,128)(2,1)} %copy.38), calls=%async_computation | async-start | bytes 524288 | tf_op jit(solution)/shard_map/all_to_all | solution.py:90
  26.8 1.3 %slice.37 = bf16[16,256,192]{1,2,0:T(8,128)(2,1)} slice(bf16[16,288,192]{1,2,0:T(8,128)(2,1)S(1)} %convert_bitcast_fusion), slice={[0:16], [0:256], [0:192]} | slice | bytes 3145728 | tf_op jit(solution)/shard_map/slice | solution.py:95
  28.0 0.0 copy-done
  28.0 0.0 copy-done.1
  28.1 0.0 copy-done.2
  28.1 0.1 fusion.59
  28.2 0.1 select_reduce_fusion
  28.3 6.0 %all-to-all-done = bf16[16,32,192]{2,1,0:T(8,128)(2,1)S(1)} async-done(((bf16[16,32,192]{2,1,0:T(8,128)(2,1)}), bf16[16,32,192]{2,1,0:T(8,128)(2,1)S(1)}, u32[]{:S(2)}, u32[]{:S(2)}) %all-to-all-start) | async-done | bytes 196640 | tf_op jit(solution)/shard_map/all_to_all | solution.py:90
  34.3 3.7 %all-to-all-start.1 = ((bf16[16,256,192]{1,2,0:T(8,128)(2,1)}), bf16[16,256,192]{1,2,0:T(8,128)(2,1)S(1)}, u32[]{:S(2)}, u32[]{:S(2)}) async-start(bf16[16,256,192]{1,2,0:T(8,128)(2,1)} %slice.37), calls=%async_computation.1 | async-start | bytes 3145728 | tf_op jit(solution)/shard_map/all_to_all | solution.py:95
  38.0 0.1 compare_and_fusion
  38.2 0.4 multiply_cosine_fusion
  38.6 0.1 convert_reduce_fusion.1
  38.7 0.1 copy.51
  38.8 0.1 copy.40
  38.8 27.9 %all-gather.1 = bf16[8,192,32]{1,2,0:T(8,128)(2,1)S(1)} all-gather(bf16[1,192,32]{1,2,0:T(8,128)(2,1)S(1)} %bitcast.75), channel_id=2, replica_groups={{0,1,2,3,4,5,6,7},{8,9,10,11,12,13,14,15},{16,17,18,19,20,21,22,23},{24..., dimensions={0}, use_global_device_ids=true | all-gather | bytes 110592 | tf_op jit(solution)/shard_map/all_gather | solution.py:92
  66.8 0.1 copy.53
  66.8 0.1 copy.52
  67.0 0.4 fusion.43
  67.4 0.0 all-to-all-done.1
  67.4 0.2 convert_reduce_fusion
  67.6 0.1 reshape.324
  67.7 0.3 fusion.60
  68.0 0.1 subtract_convert_fusion
  68.1 0.3 fusion.62
  68.4 0.1 fusion.23
  68.5 0.3 fusion.11
  68.8 0.1 copy.47
  68.9 0.7 copy.62
  (7 shorter events, 0.1 us)
Async XLA Ops:
  18.1 9.9 %copy-start = (s32[64]{0:T(128)S(1)}, s32[64]{0:T(128)}, u32[]{:S(2)}) copy-start(s32[64]{0:T(128)} %param.11) | copy-start | bytes 772
  18.1 9.9 %copy-start.1 = (s32[64]{0:T(128)S(1)}, s32[64]{0:T(128)}, u32[]{:S(2)}) copy-start(s32[64]{0:T(128)} %param.13) | copy-start | bytes 772
  18.1 9.9 %copy-start.2 = (s32[64]{0:T(128)S(1)}, s32[64]{0:T(128)}, u32[]{:S(2)}) copy-start(s32[64]{0:T(128)} %param.12) | copy-start | bytes 772
  19.2 15.1 %all-to-all-start = ((bf16[16,32,192]{2,1,0:T(8,128)(2,1)}), bf16[16,32,192]{2,1,0:T(8,128)(2,1)S(1)}, u32[]{:S(2)}, u32[]{:S(2)}) async-start(bf16[16,32,192]{2,1,0:T(8,128)(2,1)} %copy.38), calls=%async_computation | async-start | bytes 524288 | tf_op jit(solution)/shard_map/all_to_all | solution.py:90
  34.3 33.1 %all-to-all-start.1 = ((bf16[16,256,192]{1,2,0:T(8,128)(2,1)}), bf16[16,256,192]{1,2,0:T(8,128)(2,1)S(1)}, u32[]{:S(2)}, u32[]{:S(2)}) async-start(bf16[16,256,192]{1,2,0:T(8,128)(2,1)} %slice.37), calls=%async_computation.1 | async-start | bytes 3145728 | tf_op jit(solution)/shard_map/all_to_all | solution.py:95

commit v5 on v4

--- a/solution.py
+++ b/solution.py
@@ -79,20 +79,21 @@
     token_ids = jnp.arange(total_tokens, dtype=jnp.int32)
     placement = ((source[:, None] == token_ids[None, :]) & filled[:, None]).astype(jnp.bfloat16)
 
-    joined = jnp.concatenate([wq, wk, wv], axis=1)
-    term = jnp.dot(tokens, joined, preferred_element_type=jnp.float32).astype(jnp.bfloat16)
-    slot_rows = jnp.einsum(
-        "jf,csj->cfs",
-        term,
-        placement.reshape(shards, capacity, total_tokens),
-        preferred_element_type=jnp.float32,
-    ).astype(jnp.bfloat16)
-    kv_received = lax.all_to_all(slot_rows[:, q_cols:], "ctx", 0, 0, tiled=False)
+    def placed(weights):
+        term = jnp.dot(tokens, weights, preferred_element_type=jnp.float32).astype(jnp.bfloat16)
+        return jnp.einsum(
+            "jf,csj->cfs",
+            term,
+            placement.reshape(shards, capacity, total_tokens),
+            preferred_element_type=jnp.float32,
+        ).astype(jnp.bfloat16)
+
+    kv_received = lax.all_to_all(placed(jnp.concatenate([wk, wv], axis=1)), "ctx", 0, 0, tiled=False)
+    q_received = lax.all_to_all(placed(wq), "ctx", 0, 0, tiled=False)
     kv_summed = lax.optimization_barrier(jnp.sum(kv_received.astype(jnp.float32), axis=0))
     pieces = lax.all_gather(
         jnp.transpose(kv_summed).astype(jnp.bfloat16), "tp", axis=0, axis_index_groups=groups
     )
-    q_received = lax.all_to_all(slot_rows[:, :q_cols], "ctx", 0, 0, tiled=False)
     q_summed = jnp.transpose(jnp.sum(q_received.astype(jnp.float32), axis=0))
     key_unrotated = jnp.transpose(pieces[:, :, :key_value_columns], (1, 0, 2)).reshape(capacity, HEAD_SIZE)
     value_matrix = jnp.transpose(pieces[:, :, key_value_columns:], (1, 0, 2)).reshape(capacity, HEAD_SIZE)

time: 70 us -> 67.1 us (0.959)
  matrix products: 12.8 us -> 20.9 us
  waiting for transfers between devices: 6.01 us -> 0.01 us
  local copies, waits for them, and re-layouts: 6.72 us -> 2.31 us
  blocking collectives: 27.9 us -> 24.4 us
  starting transfers between devices: 11.3 us -> 14.2 us
    dot_general x2 -> x3, matrix products: 12.2 us -> 20.3 us  [the longest x2 16.9 us: placed(): jnp.einsum('jf,csj->cfs', term, placement.reshape(shards, capacity, total...]
    all_to_all x2, waiting for transfers between devices: 6.01 us -> 0.01 us  [the longest x1 0.01 us: body(): q_received = lax.all_to_all(placed(wq), 'ctx', 0, 0, tiled=False)]
    all_gather x1, blocking collectives: 27.9 us -> 24.4 us  [body(): lax.all_gather(jnp.transpose(kv_summed).astype(jnp.bfloat16), 'tp', axis=...]
    all_to_all x2, starting transfers between devices: 11.3 us -> 14.2 us  [the longest x1 7.59 us: body(): lax.all_to_all(placed(jnp.concatenate([wk, wv], axis=1)), 'ctx', 0, 0, ti...]
    slice x3 -> x0, local copies, waits for them, and re-layouts: 2.43 us -> none  [the longest x1 1.27 us: body(): q_received = lax.all_to_all(slot_rows[:, :q_cols], 'ctx', 0, 0, tiled=False)]
    unnamed x12 -> x11, local copies, waits for them, and re-layouts: 2.83 us -> 0.86 us
  transfers between devices with their start and end apart: 2 -> 2, of which waited for: 1 -> 0; matrix products, arithmetic and copies ran while one was open for 4% -> 17% of each run, Pallas kernels for 0% -> 0%
where the time goes in v5:
time: 67.1 us; the launch traced here: 66.7 us
  blocking collectives  24.4 us (36%)
  matrix products  20.9 us (31%)
  starting transfers between devices  14.2 us (21%)
  other arithmetic  4.62 us (7%)
  local copies, waits for them, and re-layouts  2.31 us (3%)
    all_gather x1, blocking collectives, body(): lax.all_gather(jnp.transpose(kv_summed).astype(jnp.bfloat16), 'tp', axis=...  24.4 us
    dot_general x2, matrix products, placed(): jnp.einsum('jf,csj->cfs', term, placement.reshape(shards, capacity, total...  16.9 us
    all_to_all x1, starting transfers between devices, body(): lax.all_to_all(placed(jnp.concatenate([wk, wv], axis=1)), 'ctx', 0, 0, ti...  7.59 us
    all_to_all x1, starting transfers between devices, body(): q_received = lax.all_to_all(placed(wq), 'ctx', 0, 0, tiled=False)  6.66 us
    dot_general x1, matrix products, placed(): jnp.dot(tokens, weights, preferred_element_type=jnp.float32)  3.44 us
  transfers between devices with their start and end apart: 2, of which 0 were waited for; matrix products, arithmetic and copies ran while one was open for 17% of the time, Pallas kernels for 0%

profile of v5, /device:TPU:1, one launch (start us, length us, event | category | flops | bytes accessed | tf_op | source)
XLA Modules:
  0.0 66.7 jit_solution(4156682595019722871)
XLA Ops:
  0.0 0.0 copy-start
  0.0 0.8 %copy.26 = s32[64,1]{1,0:T(8,128)S(1)} copy(s32[64,1]{0,1:T(1,128)} %bitcast.88) | data formatting | bytes 512 | tf_op jit(solution)/shard_map/reshape.296
  0.8 0.1 reduce-window.9
  0.9 0.1 reduce.2
  1.0 0.7 %sub.71 = s32[64]{0:T(128)S(1)} subtract(s32[64]{0:T(128)S(1)} %reduce.2, s32[64]{0:T(128)} %param.11) | non-fusion elementwise | flops 64 | bytes 768 | tf_op jit(solution)/shard_map/sub | solution.py:14
  1.7 1.1 %fusion.60 = pred[3072]{0:T(1024)(128)(4,1)S(1)} fusion(s32[64]{0:T(128)} %param.11, s32[64]{0:T(128)} %param.13, s32[3072]{0:T(1024)S(1)} %get-tuple-element.21, s32[64]{0:T(128)} %param.12, s32[3072]{0:T(1024)S(1)} %get-tuple-element.22), kind=kLoop, calls=%fused_computation.71 | loop fusion | flops 1373184 | bytes 28416 | tf_op jit(solution)/shard_map/reduce_or | solution.py:21
  2.8 1.0 %fusion.28 = s32[3072]{0:T(1024)S(1)} fusion(s32[64]{0:T(128)S(1)} %sub.71, s32[64]{0:T(128)} %param.13, s32[3072]{0:T(1024)S(1)} %get-tuple-element.21, s32[64]{0:T(128)} %param.11, s32[64]{0:T(128)} %param.12, s32[3072]{0:T(1024)S(1)} %get-tuple-element.22), kind=kLoop, calls=%fused_computation.27 | loop fusion | flops 1766400 | bytes 37888 | tf_op jit(solution)/shard_map/reduce_sum | solution.py:23
  3.8 0.1 eq.66
  3.8 0.1 and.67
  3.9 10.2 %fusion.21 = bf16[16,32,192]{2,1,0:T(8,128)(2,1)} fusion(s32[16,192]{1,0:T(8,128)S(1)} %eq.66, pred[16,192]{1,0:T(8,128)(4,1)S(1)} %and.67, bf16[2048,1024]{1,0:T(8,128)(2,1)} %param.7, bf16[1024,16]{0,1:T(8,128)(2,1)} %param.10, bf16[1024,16]{0,1:T(8,128)(2,1)} %param.9), kind=kOutput, calls=%fused_computation.21 | convolution fusion | flops 549748736 | bytes 4471808 | tf_op jit(solution)/shard_map/jf,csj->cfs/dot_general | solution.py:84
  14.1 7.6 %all-to-all-start = ((bf16[16,32,192]{2,1,0:T(8,128)(2,1)}), bf16[16,32,192]{2,1,0:T(8,128)(2,1)S(1)}, u32[]{:S(2)}, u32[]{:S(2)}) async-start(bf16[16,32,192]{2,1,0:T(8,128)(2,1)} %fusion.21), calls=%async_computation | async-start | bytes 524288 | tf_op jit(solution)/shard_map/all_to_all | solution.py:91
  21.7 0.0 copy-done
  21.7 3.4 %fusion.9.clone.5 = bf16[2048,256,1]{1,0,2:T(8,128)(2,1)S(1)} fusion(bf16[2048,1024]{1,0:T(8,128)(2,1)} %param.7, bf16[1024,256]{1,0:T(8,128)(2,1)S(1)} %copy-done), kind=kOutput, calls=%fused_computation.10.clone.clone.clone.2 | convolution fusion | flops 1074266112 | bytes 5767168 | tf_op jit(solution)/shard_map/dot_general | solution.py:83
  25.2 0.0 copy-start.1
  25.2 0.0 copy-start.2
  25.2 0.0 copy-start.3
  25.2 6.7 %fusion.14 = bf16[16,256,192]{1,2,0:T(8,128)(2,1)} fusion(s32[16,192]{1,0:T(8,128)S(1)} %eq.66, pred[16,192]{1,0:T(8,128)(4,1)S(1)} %and.67, bf16[2048,256,1]{1,0,2:T(8,128)(2,1)S(1)} %fusion.9.clone.5), kind=kOutput, calls=%fused_computation.14 | convolution fusion | flops 3234594816 | bytes 2636800 | tf_op jit(solution)/shard_map/jf,csj->cfs/dot_general | solution.py:84
  31.9 0.0 copy-done.1
  31.9 0.0 copy-done.2
  31.9 0.0 copy-done.3
  31.9 0.1 fusion.73
  32.1 0.1 select_reduce_fusion
  32.2 0.0 all-to-all-done
  32.2 6.7 %all-to-all-start.1 = ((bf16[16,256,192]{1,2,0:T(8,128)(2,1)}), bf16[16,256,192]{1,2,0:T(8,128)(2,1)S(1)}, u32[]{:S(2)}, u32[]{:S(2)}) async-start(bf16[16,256,192]{1,2,0:T(8,128)(2,1)} %fusion.14), calls=%async_computation.1 | async-start | bytes 3145728 | tf_op jit(solution)/shard_map/all_to_all | solution.py:92
  38.9 0.1 compare_and_fusion
  39.0 0.4 multiply_cosine_fusion
  39.4 0.1 convert_reduce_fusion.1
  39.5 24.4 %all-gather.1 = bf16[8,192,32]{1,2,0:T(8,128)(2,1)S(1)} all-gather(bf16[1,192,32]{1,2,0:T(8,128)(2,1)S(1)} %bitcast.87), channel_id=2, replica_groups={{0,1,2,3,4,5,6,7},{8,9,10,11,12,13,14,15},{16,17,18,19,20,21,22,23},{24..., dimensions={0}, use_global_device_ids=true | all-gather | bytes 110592 | tf_op jit(solution)/shard_map/all_gather | solution.py:94
  63.9 0.1 copy.37
  64.0 0.1 copy.38
  64.1 0.4 fusion.57
  64.6 0.0 all-to-all-done.1
  64.6 0.2 convert_reduce_fusion
  64.8 0.1 reshape.325
  64.9 0.3 fusion.74
  65.2 0.1 subtract_convert_fusion
  65.3 0.3 fusion.76
  65.6 0.1 fusion.31
  65.7 0.3 fusion.26
  66.0 0.1 copy.33
  66.1 0.7 copy.47
  (7 shorter events, 0.1 us)
Async XLA Ops:
  0.0 21.7 %copy-start = (bf16[1024,256]{1,0:T(8,128)(2,1)S(1)}, bf16[1024,256]{1,0:T(8,128)(2,1)}, u32[]{:S(2)}) copy-start(bf16[1024,256]{1,0:T(8,128)(2,1)} %param.8) | copy-start | bytes 1572868
  14.1 18.0 %all-to-all-start = ((bf16[16,32,192]{2,1,0:T(8,128)(2,1)}), bf16[16,32,192]{2,1,0:T(8,128)(2,1)S(1)}, u32[]{:S(2)}, u32[]{:S(2)}) async-start(bf16[16,32,192]{2,1,0:T(8,128)(2,1)} %fusion.21), calls=%async_computation | async-start | bytes 524288 | tf_op jit(solution)/shard_map/all_to_all | solution.py:91
  25.2 6.7 %copy-start.1 = (s32[64]{0:T(128)S(1)}, s32[64]{0:T(128)}, u32[]{:S(2)}) copy-start(s32[64]{0:T(128)} %param.11) | copy-start | bytes 772
  25.2 6.7 %copy-start.2 = (s32[64]{0:T(128)S(1)}, s32[64]{0:T(128)}, u32[]{:S(2)}) copy-start(s32[64]{0:T(128)} %param.13) | copy-start | bytes 772
  25.2 6.7 %copy-start.3 = (s32[64]{0:T(128)S(1)}, s32[64]{0:T(128)}, u32[]{:S(2)}) copy-start(s32[64]{0:T(128)} %param.12) | copy-start | bytes 772
  32.2 32.4 %all-to-all-start.1 = ((bf16[16,256,192]{1,2,0:T(8,128)(2,1)}), bf16[16,256,192]{1,2,0:T(8,128)(2,1)S(1)}, u32[]{:S(2)}, u32[]{:S(2)}) async-start(bf16[16,256,192]{1,2,0:T(8,128)(2,1)} %fusion.14), calls=%async_computation.1 | async-start | bytes 3145728 | tf_op jit(solution)/shard_map/all_to_all | solution.py:92

commit v6 on v5

--- a/solution.py
+++ b/solution.py
@@ -80,7 +80,9 @@
     placement = ((source[:, None] == token_ids[None, :]) & filled[:, None]).astype(jnp.bfloat16)
 
     def placed(weights):
-        term = jnp.dot(tokens, weights, preferred_element_type=jnp.float32).astype(jnp.bfloat16)
+        term = lax.optimization_barrier(
+            jnp.dot(tokens, weights, preferred_element_type=jnp.float32).astype(jnp.bfloat16)
+        )
         return jnp.einsum(
             "jf,csj->cfs",
             term,

time: 67.1 us -> 67.5 us (level)
    dot_general x1 -> x2, matrix products: 3.44 us -> 7 us  [placed(): jnp.dot(tokens, weights, preferred_element_type=jnp.float32)]
    dot_general x2, matrix products: 16.9 us -> 13.7 us  [placed(): jnp.einsum('jf,csj->cfs', term, placement.reshape(shards, capacity, total...]
where the time goes in v6:
time: 67.5 us; the launch traced here: 67.1 us
  blocking collectives  24.4 us (36%)
  matrix products  21.3 us (32%)
  starting transfers between devices  14.2 us (21%)
  other arithmetic  4.62 us (7%)
  local copies, waits for them, and re-layouts  2.31 us (3%)
    all_gather x1, blocking collectives, body(): lax.all_gather(jnp.transpose(kv_summed).astype(jnp.bfloat16), 'tp', axis=...  24.4 us
    dot_general x2, matrix products, placed(): jnp.einsum('jf,csj->cfs', term, placement.reshape(shards, capacity, total...  13.7 us
    all_to_all x1, starting transfers between devices, body(): lax.all_to_all(placed(jnp.concatenate([wk, wv], axis=1)), 'ctx', 0, 0, ti...  7.59 us
    dot_general x2, matrix products, placed(): jnp.dot(tokens, weights, preferred_element_type=jnp.float32)  7 us
    all_to_all x1, starting transfers between devices, body(): q_received = lax.all_to_all(placed(wq), 'ctx', 0, 0, tiled=False)  6.66 us
  transfers between devices with their start and end apart: 2, of which 0 were waited for; matrix products, arithmetic and copies ran while one was open for 17% of the time, Pallas kernels for 0%

profile of v6, /device:TPU:1, one launch (start us, length us, event | category | flops | bytes accessed | tf_op | source)
XLA Modules:
  0.0 67.1 jit_solution(17294708530912527922)
XLA Ops:
  0.0 0.0 copy-start
  0.0 0.8 %copy.26 = s32[64,1]{1,0:T(8,128)S(1)} copy(s32[64,1]{0,1:T(1,128)} %bitcast.73) | data formatting | bytes 512 | tf_op jit(solution)/shard_map/reshape.296
  0.8 0.1 reduce-window.9
  0.9 0.1 reduce.2
  1.0 0.7 sub.71
  1.7 1.1 %fusion.58 = pred[3072]{0:T(1024)(128)(4,1)S(1)} fusion(s32[64]{0:T(128)} %param.11, s32[64]{0:T(128)} %param.13, s32[3072]{0:T(1024)S(1)} %get-tuple-element.21, s32[64]{0:T(128)} %param.12, s32[3072]{0:T(1024)S(1)} %get-tuple-element.22), kind=kLoop, calls=%fused_computation.72 | loop fusion | flops 1373184 | bytes 28416 | tf_op jit(solution)/shard_map/reduce_or | solution.py:21
  2.8 1.0 %fusion.28 = s32[3072]{0:T(1024)S(1)} fusion(s32[64]{0:T(128)S(1)} %sub.71, s32[64]{0:T(128)} %param.13, s32[3072]{0:T(1024)S(1)} %get-tuple-element.21, s32[64]{0:T(128)} %param.11, s32[64]{0:T(128)} %param.12, s32[3072]{0:T(1024)S(1)} %get-tuple-element.22), kind=kLoop, calls=%fused_computation.27 | loop fusion | flops 1766400 | bytes 37888 | tf_op jit(solution)/shard_map/reduce_sum | solution.py:23
  3.8 0.1 eq.66
  3.8 0.1 and.67
  3.9 3.6 %fusion.9 = bf16[2048,32]{0,1:T(8,128)(2,1)S(1)} fusion(bf16[2048,1024]{1,0:T(8,128)(2,1)} %param.7, bf16[1024,16]{0,1:T(8,128)(2,1)} %param.10, bf16[1024,16]{0,1:T(8,128)(2,1)} %param.9), kind=kOutput, calls=%fused_computation.11 | convolution fusion | flops 134414336 | bytes 4390912 | tf_op jit(solution)/shard_map/dot_general | solution.py:84
  7.5 7.1 %fusion.20 = bf16[16,32,192]{2,1,0:T(8,128)(2,1)} fusion(s32[16,192]{1,0:T(8,128)S(1)} %eq.66, pred[16,192]{1,0:T(8,128)(4,1)S(1)} %and.67, bf16[2048,32]{0,1:T(8,128)(2,1)S(1)} %fusion.9), kind=kOutput, calls=%fused_computation.20 | convolution fusion | flops 415334400 | bytes 343040 | tf_op jit(solution)/shard_map/jf,csj->cfs/dot_general | solution.py:86
  14.6 7.6 %all-to-all-start = ((bf16[16,32,192]{2,1,0:T(8,128)(2,1)}), bf16[16,32,192]{2,1,0:T(8,128)(2,1)S(1)}, u32[]{:S(2)}, u32[]{:S(2)}) async-start(bf16[16,32,192]{2,1,0:T(8,128)(2,1)} %fusion.20), calls=%async_computation | async-start | bytes 524288 | tf_op jit(solution)/shard_map/all_to_all | solution.py:93
  22.2 0.0 copy-done
  22.2 3.4 %convolution_convert_fusion = bf16[2048,256]{1,0:T(8,128)(2,1)S(1)} fusion(bf16[2048,1024]{1,0:T(8,128)(2,1)} %param.7, bf16[1024,256]{1,0:T(8,128)(2,1)S(1)} %copy-done), kind=kOutput, calls=%fused_computation.9 | convolution fusion | flops 1074266112 | bytes 5767168 | tf_op jit(solution)/shard_map/dot_general | solution.py:84
  25.6 0.0 copy-start.1
  25.6 0.0 copy-start.2
  25.6 0.0 copy-start.3
  25.7 6.7 %fusion.13 = bf16[16,256,192]{1,2,0:T(8,128)(2,1)} fusion(s32[16,192]{1,0:T(8,128)S(1)} %eq.66, pred[16,192]{1,0:T(8,128)(4,1)S(1)} %and.67, bf16[2048,256]{1,0:T(8,128)(2,1)S(1)} %convolution_convert_fusion), kind=kOutput, calls=%fused_computation.13 | convolution fusion | flops 3234594816 | bytes 2636800 | tf_op jit(solution)/shard_map/jf,csj->cfs/dot_general | solution.py:86
  32.3 0.0 copy-done.1
  32.3 0.0 copy-done.2
  32.3 0.0 copy-done.3
  32.4 0.1 fusion.70
  32.5 0.1 select_reduce_fusion
  32.6 0.0 all-to-all-done
  32.6 6.7 %all-to-all-start.1 = ((bf16[16,256,192]{1,2,0:T(8,128)(2,1)}), bf16[16,256,192]{1,2,0:T(8,128)(2,1)S(1)}, u32[]{:S(2)}, u32[]{:S(2)}) async-start(bf16[16,256,192]{1,2,0:T(8,128)(2,1)} %fusion.13), calls=%async_computation.1 | async-start | bytes 3145728 | tf_op jit(solution)/shard_map/all_to_all | solution.py:94
  39.3 0.1 compare_and_fusion
  39.4 0.4 multiply_cosine_fusion
  39.9 0.1 convert_reduce_fusion.1
  39.9 24.4 %all-gather.1 = bf16[8,192,32]{1,2,0:T(8,128)(2,1)S(1)} all-gather(bf16[1,192,32]{1,2,0:T(8,128)(2,1)S(1)} %bitcast.72), channel_id=2, replica_groups={{0,1,2,3,4,5,6,7},{8,9,10,11,12,13,14,15},{16,17,18,19,20,21,22,23},{24..., dimensions={0}, use_global_device_ids=true | all-gather | bytes 110592 | tf_op jit(solution)/shard_map/all_gather | solution.py:96
  64.3 0.1 copy.37
  64.4 0.1 copy.38
  64.5 0.4 fusion.55
  65.0 0.0 all-to-all-done.1
  65.0 0.2 convert_reduce_fusion
  65.2 0.1 reshape.325
  65.3 0.3 fusion.71
  65.6 0.1 subtract_convert_fusion
  65.7 0.3 fusion.73
  66.0 0.1 fusion.31
  66.1 0.3 fusion.25
  66.4 0.1 copy.33
  66.5 0.7 copy.47
  (7 shorter events, 0.1 us)
Async XLA Ops:
  0.0 22.2 %copy-start = (bf16[1024,256]{1,0:T(8,128)(2,1)S(1)}, bf16[1024,256]{1,0:T(8,128)(2,1)}, u32[]{:S(2)}) copy-start(bf16[1024,256]{1,0:T(8,128)(2,1)} %param.8) | copy-start | bytes 1572868
  14.6 18.0 %all-to-all-start = ((bf16[16,32,192]{2,1,0:T(8,128)(2,1)}), bf16[16,32,192]{2,1,0:T(8,128)(2,1)S(1)}, u32[]{:S(2)}, u32[]{:S(2)}) async-start(bf16[16,32,192]{2,1,0:T(8,128)(2,1)} %fusion.20), calls=%async_computation | async-start | bytes 524288 | tf_op jit(solution)/shard_map/all_to_all | solution.py:93
  25.6 6.7 %copy-start.1 = (s32[64]{0:T(128)S(1)}, s32[64]{0:T(128)}, u32[]{:S(2)}) copy-start(s32[64]{0:T(128)} %param.11) | copy-start | bytes 772
  25.6 6.7 %copy-start.2 = (s32[64]{0:T(128)S(1)}, s32[64]{0:T(128)}, u32[]{:S(2)}) copy-start(s32[64]{0:T(128)} %param.13) | copy-start | bytes 772
  25.6 6.7 %copy-start.3 = (s32[64]{0:T(128)S(1)}, s32[64]{0:T(128)}, u32[]{:S(2)}) copy-start(s32[64]{0:T(128)} %param.12) | copy-start | bytes 772
  32.6 32.4 %all-to-all-start.1 = ((bf16[16,256,192]{1,2,0:T(8,128)(2,1)}), bf16[16,256,192]{1,2,0:T(8,128)(2,1)S(1)}, u32[]{:S(2)}, u32[]{:S(2)}) async-start(bf16[16,256,192]{1,2,0:T(8,128)(2,1)} %fusion.13), calls=%async_computation.1 | async-start | bytes 3145728 | tf_op jit(solution)/shard_map/all_to_all | solution.py:94

commit v7 on v6

--- a/solution.py
+++ b/solution.py
@@ -10,8 +10,8 @@
 
 
 def slot_table(slot_ids, doc_len, doc_shard, doc_slot, capacity):
-    ends = jnp.cumsum(doc_len)
-    starts = ends - doc_len
+    doc_ids = jnp.arange(doc_len.shape[0], dtype=jnp.int32)
+    starts = jnp.sum(jnp.where(doc_ids[None, :] < doc_ids[:, None], doc_len[None, :], 0), axis=1)
     shard_of = slot_ids // capacity
     local = slot_ids % capacity
     offset = local[:, None] - doc_slot[None, :]
@@ -21,7 +21,6 @@
     filled = jnp.any(match, axis=1)
     position = jnp.sum(jnp.where(match, offset, 0), axis=1)
     source = jnp.sum(jnp.where(match, starts[None, :] + offset, 0), axis=1)
-    doc_ids = jnp.arange(doc_len.shape[0], dtype=jnp.int32)
     doc_of = jnp.sum(jnp.where(match, doc_ids[None, :], 0), axis=1)
     slot_doc = jnp.where(filled, doc_of, -1 - slot_ids)
     return (source, filled, slot_doc, position)
@@ -77,7 +76,8 @@
         jnp.arange(slot_total, dtype=jnp.int32), doc_len, doc_shard, doc_slot, capacity
     )
     token_ids = jnp.arange(total_tokens, dtype=jnp.int32)
-    placement = ((source[:, None] == token_ids[None, :]) & filled[:, None]).astype(jnp.bfloat16)
+    source = jnp.where(filled, source, -1)
+    placement = (source[:, None] == token_ids[None, :]).astype(jnp.bfloat16)
 
     def placed(weights):
         term = lax.optimization_barrier(

time: 67.5 us -> 64.3 us (0.953)
  matrix products: 21.3 us -> 19.1 us
  local copies, waits for them, and re-layouts: 2.31 us -> 1.42 us
    dot_general x2, matrix products: 13.7 us -> 11.5 us  [placed(): jnp.einsum('jf,csj->cfs', term, placement.reshape(shards, capacity, total...]
    reduce_sum x0 -> x1, other arithmetic: none -> 0.82 us  [slot_table(): jnp.sum(jnp.where(doc_ids[None, :] < doc_ids[:, None], doc_len[None, :],...]
    another operation x1 -> x0, local copies, waits for them, and re-layouts: 0.8 us -> none
  transfers between devices with their start and end apart: 2 -> 2, of which waited for: 0 -> 0; matrix products, arithmetic and copies ran while one was open for 17% -> 16% of each run, Pallas kernels for 0% -> 0%
where the time goes in v7:
time: 64.3 us; the launch traced here: 63.9 us
  blocking collectives  24.4 us (38%)
  matrix products  19.1 us (30%)
  starting transfers between devices  14.2 us (22%)
  other arithmetic  4.59 us (7%)
  local copies, waits for them, and re-layouts  1.42 us (2%)
    all_gather x1, blocking collectives, body(): lax.all_gather(jnp.transpose(kv_summed).astype(jnp.bfloat16), 'tp', axis=...  24.4 us
    dot_general x2, matrix products, placed(): jnp.einsum('jf,csj->cfs', term, placement.reshape(shards, capacity, total...  11.5 us
    all_to_all x1, starting transfers between devices, body(): lax.all_to_all(placed(jnp.concatenate([wk, wv], axis=1)), 'ctx', 0, 0, ti...  7.58 us
    dot_general x2, matrix products, placed(): jnp.dot(tokens, weights, preferred_element_type=jnp.float32)  6.99 us
    all_to_all x1, starting transfers between devices, body(): q_received = lax.all_to_all(placed(wq), 'ctx', 0, 0, tiled=False)  6.66 us
  transfers between devices with their start and end apart: 2, of which 0 were waited for; matrix products, arithmetic and copies ran while one was open for 16% of the time, Pallas kernels for 0%

profile of v7, /device:TPU:1, one launch (start us, length us, event | category | flops | bytes accessed | tf_op | source)
XLA Modules:
  0.0 63.9 jit_solution(13097482461823263878)
XLA Ops:
  0.0 0.0 copy-start
  0.0 0.8 %select_reduce_fusion.1 = s32[64]{0:T(128)S(1)} fusion(s32[64]{0:T(128)} %param.11), kind=kLoop, calls=%fused_computation.70 | loop fusion | flops 12224 | bytes 512 | tf_op jit(solution)/shard_map/reduce_sum | solution.py:14
  0.8 1.1 %fusion.45 = pred[3072]{0:T(1024)(128)(4,1)S(1)} fusion(s32[64]{0:T(128)} %param.11, s32[64]{0:T(128)} %param.13, s32[3072]{0:T(1024)S(1)} %get-tuple-element.21, s32[64]{0:T(128)} %param.12, s32[3072]{0:T(1024)S(1)} %get-tuple-element.22), kind=kLoop, calls=%fused_computation.69 | loop fusion | flops 1373184 | bytes 28416 | tf_op jit(solution)/shard_map/reduce_or | solution.py:21
  1.9 1.0 %fusion.15 = s32[3072]{0:T(1024)S(1)} fusion(s32[64]{0:T(128)S(1)} %select_reduce_fusion.1, s32[64]{0:T(128)} %param.13, s32[3072]{0:T(1024)S(1)} %get-tuple-element.21, s32[64]{0:T(128)} %param.11, s32[64]{0:T(128)} %param.12, s32[3072]{0:T(1024)S(1)} %get-tuple-element.22), kind=kLoop, calls=%fused_computation.24 | loop fusion | flops 1766400 | bytes 37888 | tf_op jit(solution)/shard_map/reduce_sum | solution.py:23
  2.9 0.1 select_n.86
  3.0 3.6 %fusion.4 = bf16[2048,32]{0,1:T(8,128)(2,1)S(1)} fusion(bf16[2048,1024]{1,0:T(8,128)(2,1)} %param.7, bf16[1024,16]{0,1:T(8,128)(2,1)} %param.10, bf16[1024,16]{0,1:T(8,128)(2,1)} %param.9), kind=kOutput, calls=%fused_computation.8 | convolution fusion | flops 134414336 | bytes 4390912 | tf_op jit(solution)/shard_map/dot_general | solution.py:84
  6.6 6.1 %fusion.9 = bf16[16,32,192]{2,1,0:T(8,128)(2,1)} fusion(s32[16,192]{1,0:T(8,128)S(1)} %select_n.86, bf16[2048,32]{0,1:T(8,128)(2,1)S(1)} %fusion.4), kind=kOutput, calls=%fused_computation.17 | convolution fusion | flops 409042944 | bytes 339968 | tf_op jit(solution)/shard_map/jf,csj->cfs/dot_general | solution.py:86
  12.6 7.6 %all-to-all-start = ((bf16[16,32,192]{2,1,0:T(8,128)(2,1)}), bf16[16,32,192]{2,1,0:T(8,128)(2,1)S(1)}, u32[]{:S(2)}, u32[]{:S(2)}) async-start(bf16[16,32,192]{2,1,0:T(8,128)(2,1)} %fusion.9), calls=%async_computation | async-start | bytes 524288 | tf_op jit(solution)/shard_map/all_to_all | solution.py:93
  20.2 0.0 copy-done
  20.2 3.4 %convolution_convert_fusion = bf16[2048,256]{1,0:T(8,128)(2,1)S(1)} fusion(bf16[2048,1024]{1,0:T(8,128)(2,1)} %param.7, bf16[1024,256]{1,0:T(8,128)(2,1)S(1)} %copy-done), kind=kOutput, calls=%fused_computation.6 | convolution fusion | flops 1074266112 | bytes 5767168 | tf_op jit(solution)/shard_map/dot_general | solution.py:84
  23.7 0.0 copy-start.1
  23.7 0.0 copy-start.2
  23.7 0.0 copy-start.3
  23.7 5.4 %fusion.6 = bf16[16,256,192]{1,2,0:T(8,128)(2,1)} fusion(s32[16,192]{1,0:T(8,128)S(1)} %select_n.86, bf16[2048,256]{1,0:T(8,128)(2,1)S(1)} %convolution_convert_fusion), kind=kOutput, calls=%fused_computation.10 | convolution fusion | flops 3228303360 | bytes 2633728 | tf_op jit(solution)/shard_map/jf,csj->cfs/dot_general | solution.py:86
  29.1 0.0 copy-done.1
  29.1 0.0 copy-done.2
  29.1 0.0 copy-done.3
  29.2 0.1 fusion.57
  29.3 0.1 select_reduce_fusion
  29.4 0.0 all-to-all-done
  29.4 6.7 %all-to-all-start.1 = ((bf16[16,256,192]{1,2,0:T(8,128)(2,1)}), bf16[16,256,192]{1,2,0:T(8,128)(2,1)S(1)}, u32[]{:S(2)}, u32[]{:S(2)}) async-start(bf16[16,256,192]{1,2,0:T(8,128)(2,1)} %fusion.6), calls=%async_computation.1 | async-start | bytes 3145728 | tf_op jit(solution)/shard_map/all_to_all | solution.py:94
  36.1 0.1 compare_and_fusion
  36.2 0.4 multiply_cosine_fusion
  36.7 0.1 convert_reduce_fusion.1
  36.7 24.4 %all-gather.1 = bf16[8,192,32]{1,2,0:T(8,128)(2,1)S(1)} all-gather(bf16[1,192,32]{1,2,0:T(8,128)(2,1)S(1)} %bitcast.71), channel_id=2, replica_groups={{0,1,2,3,4,5,6,7},{8,9,10,11,12,13,14,15},{16,17,18,19,20,21,22,23},{24..., dimensions={0}, use_global_device_ids=true | all-gather | bytes 110592 | tf_op jit(solution)/shard_map/all_gather | solution.py:96
  61.1 0.1 copy.34
  61.2 0.1 copy.33
  61.3 0.4 fusion.42
  61.8 0.0 all-to-all-done.1
  61.8 0.2 convert_reduce_fusion
  62.0 0.1 reshape.299
  62.1 0.3 fusion.58
  62.4 0.1 subtract_convert_fusion
  62.5 0.3 fusion.60
  62.8 0.1 fusion.18
  62.9 0.3 fusion.12
  63.2 0.1 copy.29
  63.3 0.7 %copy.43 = bf16[24,8,2,128]{3,1,2,0:T(8,128)(2,1)} copy(bf16[24,8,2,128]{3,2,1,0:T(2,128)(2,1)S(1)} %bitcast.69) | data formatting | bytes 196608
  (8 shorter events, 0.1 us)
Async XLA Ops:
  0.0 20.2 %copy-start = (bf16[1024,256]{1,0:T(8,128)(2,1)S(1)}, bf16[1024,256]{1,0:T(8,128)(2,1)}, u32[]{:S(2)}) copy-start(bf16[1024,256]{1,0:T(8,128)(2,1)} %param.8) | copy-start | bytes 1572868
  12.6 16.7 %all-to-all-start = ((bf16[16,32,192]{2,1,0:T(8,128)(2,1)}), bf16[16,32,192]{2,1,0:T(8,128)(2,1)S(1)}, u32[]{:S(2)}, u32[]{:S(2)}) async-start(bf16[16,32,192]{2,1,0:T(8,128)(2,1)} %fusion.9), calls=%async_computation | async-start | bytes 524288 | tf_op jit(solution)/shard_map/all_to_all | solution.py:93
  23.7 5.4 %copy-start.1 = (s32[64]{0:T(128)S(1)}, s32[64]{0:T(128)}, u32[]{:S(2)}) copy-start(s32[64]{0:T(128)} %param.11) | copy-start | bytes 772
  23.7 5.4 %copy-start.2 = (s32[64]{0:T(128)S(1)}, s32[64]{0:T(128)}, u32[]{:S(2)}) copy-start(s32[64]{0:T(128)} %param.13) | copy-start | bytes 772
  23.7 5.4 %copy-start.3 = (s32[64]{0:T(128)S(1)}, s32[64]{0:T(128)}, u32[]{:S(2)}) copy-start(s32[64]{0:T(128)} %param.12) | copy-start | bytes 772
  29.4 32.4 %all-to-all-start.1 = ((bf16[16,256,192]{1,2,0:T(8,128)(2,1)}), bf16[16,256,192]{1,2,0:T(8,128)(2,1)S(1)}, u32[]{:S(2)}, u32[]{:S(2)}) async-start(bf16[16,256,192]{1,2,0:T(8,128)(2,1)} %fusion.6), calls=%async_computation.1 | async-start | bytes 3145728 | tf_op jit(solution)/shard_map/all_to_all | solution.py:94

commit v8 on v7

--- a/solution.py
+++ b/solution.py
@@ -90,17 +90,20 @@
             preferred_element_type=jnp.float32,
         ).astype(jnp.bfloat16)
 
-    kv_received = lax.all_to_all(placed(jnp.concatenate([wk, wv], axis=1)), "ctx", 0, 0, tiled=False)
+    kv_term = jnp.dot(
+        tokens, jnp.concatenate([wk, wv], axis=1), preferred_element_type=jnp.float32
+    ).astype(jnp.bfloat16)
+    kv_full = lax.psum(kv_term, "ctx")
     q_received = lax.all_to_all(placed(wq), "ctx", 0, 0, tiled=False)
-    kv_summed = lax.optimization_barrier(jnp.sum(kv_received.astype(jnp.float32), axis=0))
-    pieces = lax.all_gather(
-        jnp.transpose(kv_summed).astype(jnp.bfloat16), "tp", axis=0, axis_index_groups=groups
-    )
+    shard = lax.axis_index("ctx")
+    my_source = lax.dynamic_slice_in_dim(source, shard * capacity, capacity)
+    mine = (my_source[:, None] == token_ids[None, :]).astype(jnp.bfloat16)
+    kv_mine = jnp.dot(mine, kv_full, preferred_element_type=jnp.float32).astype(jnp.bfloat16)
+    pieces = lax.all_gather(kv_mine, "tp", axis=0, axis_index_groups=groups)
     q_summed = jnp.transpose(jnp.sum(q_received.astype(jnp.float32), axis=0))
     key_unrotated = jnp.transpose(pieces[:, :, :key_value_columns], (1, 0, 2)).reshape(capacity, HEAD_SIZE)
     value_matrix = jnp.transpose(pieces[:, :, key_value_columns:], (1, 0, 2)).reshape(capacity, HEAD_SIZE)
 
-    shard = lax.axis_index("ctx")
     my_slots = shard * capacity + jnp.arange(capacity, dtype=jnp.int32)
     _, _, my_doc, my_pos = slot_table(my_slots, doc_len, doc_shard, doc_slot, capacity)
     heads_here = q_cols // HEAD_SIZE

time: 64.3 us -> 206 us (3.20)
  waiting for transfers between devices: 0.01 us -> 149 us
  between operations: 0.23 us -> 13.6 us
  blocking collectives: 24.4 us -> 16.2 us
  starting transfers between devices: 14.2 us -> 7.63 us
  matrix products: 19.1 us -> 15 us
  other arithmetic: 4.59 us -> 2.45 us
    psum x0 -> x1, waiting for transfers between devices: none -> 149 us  [body(): kv_full = lax.psum(kv_term, 'ctx')]
    all_gather x1, blocking collectives: 24.4 us -> 16.2 us  [body(): pieces = lax.all_gather(kv_mine, 'tp', axis=0, axis_index_groups=groups)]
    all_to_all x1 -> x0, starting transfers between devices: 7.58 us -> none  [body(): lax.all_to_all(placed(jnp.concatenate([wk, wv], axis=1)), 'ctx', 0, 0, ti...]
    dot_general x2 -> x1, matrix products: 11.5 us -> 5.39 us  [placed(): jnp.einsum('jf,csj->cfs', term, placement.reshape(shards, capacity, total...]
    dot_general x0 -> x2, matrix products: none -> 5.6 us  [the longest x1 4.27 us: body(): jnp.dot(tokens, jnp.concatenate([wk, wv], axis=1), preferred_element_type...]
    dot_general x2 -> x1, matrix products: 6.99 us -> 3.44 us  [placed(): jnp.dot(tokens, weights, preferred_element_type=jnp.float32)]
  transfers between devices with their start and end apart: 2 -> 2, of which waited for: 0 -> 1; matrix products, arithmetic and copies ran while one was open for 16% -> 6% of each run, Pallas kernels for 0% -> 0%
where the time goes in v8:
time: 206 us; the launch traced here: 205 us
  waiting for transfers between devices  149 us (72%)
  blocking collectives  16.2 us (8%)
  matrix products  15 us (7%)
  between operations  13.6 us (7%)
  starting transfers between devices  7.63 us (4%)
  other arithmetic  2.45 us (1%)
    psum x1, waiting for transfers between devices, body(): kv_full = lax.psum(kv_term, 'ctx')  149 us
    all_gather x1, blocking collectives, body(): pieces = lax.all_gather(kv_mine, 'tp', axis=0, axis_index_groups=groups)  16.2 us
    all_to_all x1, starting transfers between devices, body(): q_received = lax.all_to_all(placed(wq), 'ctx', 0, 0, tiled=False)  7.59 us
    dot_general x1, matrix products, placed(): jnp.einsum('jf,csj->cfs', term, placement.reshape(shards, capacity, total...  5.39 us
    dot_general x1, matrix products, body(): jnp.dot(tokens, jnp.concatenate([wk, wv], axis=1), preferred_element_type...  4.27 us
  transfers between devices with their start and end apart: 2, of which 1 were waited for; matrix products, arithmetic and copies ran while one was open for 6% of the time, Pallas kernels for 0%

profile of v8, /device:TPU:1, one launch (start us, length us, event | category | flops | bytes accessed | tf_op | source)
XLA Modules:
  0.0 205.3 jit_solution(4319393342468039067)
XLA Ops:
  6.5 0.0 copy-start
  6.5 0.0 copy-start.1
  6.5 0.0 copy-start.2
  6.5 0.0 copy-start.3
  6.5 0.0 all-reduce.2.cloned.1.call-start
  6.6 4.3 %fusion.2 = bf16[2048,32]{0,1:T(8,128)(2,1)} fusion(bf16[2048,1024]{1,0:T(8,128)(2,1)} %param.7, bf16[1024,16]{0,1:T(8,128)(2,1)} %param.10, bf16[1024,16]{0,1:T(8,128)(2,1)} %param.9), kind=kOutput, calls=%fused_computation.6 | convolution fusion | flops 134414336 | bytes 4390912 | tf_op jit(solution)/shard_map/dot_general | solution.py:93
  10.9 0.0 all-reduce.2.cloned.1.call-update
  10.9 0.0 copy-done.1
  10.9 0.1 select_reduce_fusion.1
  11.0 0.0 copy-done.2
  11.0 0.0 copy-done.3
  11.0 0.4 fusion.44
  11.4 0.3 fusion.14
  11.8 0.1 select_n.95
  11.8 0.0 copy-done
  11.8 3.4 %convolution_convert_fusion = bf16[2048,256]{1,0:T(8,128)(2,1)S(1)} fusion(bf16[2048,1024]{1,0:T(8,128)(2,1)} %param.7, bf16[1024,256]{1,0:T(8,128)(2,1)S(1)} %copy-done), kind=kOutput, calls=%fused_computation.4 | convolution fusion | flops 1074266112 | bytes 5767168 | tf_op jit(solution)/shard_map/dot_general | solution.py:84
  15.3 5.4 %fusion.5 = bf16[16,256,192]{1,2,0:T(8,128)(2,1)} fusion(s32[16,192]{1,0:T(8,128)S(1)} %select_n.95, bf16[2048,256]{1,0:T(8,128)(2,1)S(1)} %convolution_convert_fusion), kind=kOutput, calls=%fused_computation.10 | convolution fusion | flops 3228303360 | bytes 2633728 | tf_op jit(solution)/shard_map/jf,csj->cfs/dot_general | solution.py:86
  20.7 7.6 %all-to-all-start = ((bf16[16,256,192]{1,2,0:T(8,128)(2,1)}), bf16[16,256,192]{1,2,0:T(8,128)(2,1)S(1)}, u32[]{:S(2)}, u32[]{:S(2)}) async-start(bf16[16,256,192]{1,2,0:T(8,128)(2,1)} %fusion.5), calls=%async_computation | async-start | bytes 3145728 | tf_op jit(solution)/shard_map/all_to_all | solution.py:97
  28.3 0.1 select_reduce_fusion
  28.4 0.1 fusion.56
  28.5 0.1 dynamic_slice.3
  28.6 0.4 multiply_cosine_fusion
  29.1 0.1 compare_and_fusion
  29.2 148.9 %all-reduce.2.cloned.1.call-done = bf16[2048,32]{0,1:T(8,128)(2,1)} async-done(((bf16[2048,32]{0,1:T(8,128)(2,1)}), bf16[2048,32]{0,1:T(8,128)(2,1)}) %all-reduce.2.cloned.1.call-update) | async-done | bytes 131088 | tf_op jit(solution)/shard_map/psum | solution.py:96
  178.1 1.3 fusion.9
  179.5 16.2 %all-gather.1 = bf16[8,192,32]{1,2,0:T(8,128)(2,1)S(1)} all-gather(bf16[1,192,32]{1,2,0:T(8,128)(2,1)S(1)} %fusion.9), channel_id=2, replica_groups={{0,1,2,3,4,5,6,7},{8,9,10,11,12,13,14,15},{16,17,18,19,20,21,22,23},{24..., dimensions={0}, use_global_device_ids=true | all-gather | bytes 110592 | tf_op jit(solution)/shard_map/all_gather | solution.py:102
  195.7 0.1 copy.43
  195.8 0.1 copy.42
  195.9 0.4 fusion.41
  196.3 0.0 all-to-all-done
  196.4 0.2 convert_reduce_fusion
  196.6 0.1 reshape.299
  196.7 0.3 fusion.57
  197.0 0.1 subtract_convert_fusion
  197.0 0.3 fusion.59
  197.4 0.1 fusion.18
  197.4 0.3 fusion.11
  197.7 0.1 copy.38
  197.8 0.7 copy.52
  (8 shorter events, 0.1 us)
Async XLA Ops:
  6.5 5.3 %copy-start = (bf16[1024,256]{1,0:T(8,128)(2,1)S(1)}, bf16[1024,256]{1,0:T(8,128)(2,1)}, u32[]{:S(2)}) copy-start(bf16[1024,256]{1,0:T(8,128)(2,1)} %param.8) | copy-start | bytes 1572868
  6.5 4.4 %copy-start.1 = (s32[64]{0:T(128)S(1)}, s32[64]{0:T(128)}, u32[]{:S(2)}) copy-start(s32[64]{0:T(128)} %param.11) | copy-start | bytes 772
  6.5 4.5 %copy-start.2 = (s32[64]{0:T(128)S(1)}, s32[64]{0:T(128)}, u32[]{:S(2)}) copy-start(s32[64]{0:T(128)} %param.13) | copy-start | bytes 772
  6.5 4.5 %copy-start.3 = (s32[64]{0:T(128)S(1)}, s32[64]{0:T(128)}, u32[]{:S(2)}) copy-start(s32[64]{0:T(128)} %param.12) | copy-start | bytes 772
  6.5 171.6 %all-reduce.2.cloned.1.call-start = ((), (), s32[]{:S(2)}) async-start(), calls=%async_computation.1 | async-start | bytes 262144 | tf_op jit(solution)/shard_map/psum | solution.py:96
  20.7 175.7 %all-to-all-start = ((bf16[16,256,192]{1,2,0:T(8,128)(2,1)}), bf16[16,256,192]{1,2,0:T(8,128)(2,1)S(1)}, u32[]{:S(2)}, u32[]{:S(2)}) async-start(bf16[16,256,192]{1,2,0:T(8,128)(2,1)} %fusion.5), calls=%async_computation | async-start | bytes 3145728 | tf_op jit(solution)/shard_map/all_to_all | solution.py:97
Sparse Core Ops, SparseCore 0:
  11.0 167.0 all-reduce.1

commit v9 on v7

--- a/solution.py
+++ b/solution.py
@@ -77,7 +77,9 @@
     )
     token_ids = jnp.arange(total_tokens, dtype=jnp.int32)
     source = jnp.where(filled, source, -1)
-    placement = (source[:, None] == token_ids[None, :]).astype(jnp.bfloat16)
+    placement = (
+        source.astype(jnp.float32)[:, None] == token_ids.astype(jnp.float32)[None, :]
+    ).astype(jnp.bfloat16)
 
     def placed(weights):
         term = lax.optimization_barrier(

time: 64.3 us -> 62.9 us (0.978)
  matrix products: 19.1 us -> 17.7 us
    dot_general x2, matrix products: 11.5 us -> 10.1 us  [placed(): jnp.einsum('jf,csj->cfs', term, placement.reshape(shards, capacity, total...]
where the time goes in v9:
time: 62.9 us; the launch traced here: 62.6 us
  blocking collectives  24.4 us (39%)
  matrix products  17.7 us (28%)
  starting transfers between devices  14.2 us (23%)
  other arithmetic  4.59 us (7%)
  local copies, waits for them, and re-layouts  1.42 us (2%)
    all_gather x1, blocking collectives, body(): lax.all_gather(jnp.transpose(kv_summed).astype(jnp.bfloat16), 'tp', axis=...  24.4 us
    dot_general x2, matrix products, placed(): jnp.einsum('jf,csj->cfs', term, placement.reshape(shards, capacity, total...  10.1 us
    all_to_all x1, starting transfers between devices, body(): lax.all_to_all(placed(jnp.concatenate([wk, wv], axis=1)), 'ctx', 0, 0, ti...  7.58 us
    dot_general x2, matrix products, placed(): jnp.dot(tokens, weights, preferred_element_type=jnp.float32)  6.99 us
    all_to_all x1, starting transfers between devices, body(): q_received = lax.all_to_all(placed(wq), 'ctx', 0, 0, tiled=False)  6.66 us
  transfers between devices with their start and end apart: 2, of which 0 were waited for; matrix products, arithmetic and copies ran while one was open for 16% of the time, Pallas kernels for 0%

profile of v9, /device:TPU:1, one launch (start us, length us, event | category | flops | bytes accessed | tf_op | source)
XLA Modules:
  0.0 62.6 jit_solution(8592717496020217752)
XLA Ops:
  0.0 0.0 copy-start
  0.0 0.8 %select_reduce_fusion.1 = s32[64]{0:T(128)S(1)} fusion(s32[64]{0:T(128)} %param.11), kind=kLoop, calls=%fused_computation.73 | loop fusion | flops 12224 | bytes 512 | tf_op jit(solution)/shard_map/reduce_sum | solution.py:14
  0.8 1.1 %fusion.57 = pred[3072]{0:T(1024)(128)(4,1)S(1)} fusion(s32[64]{0:T(128)} %param.11, s32[64]{0:T(128)} %param.13, s32[3072]{0:T(1024)S(1)} %get-tuple-element.21, s32[64]{0:T(128)} %param.12, s32[3072]{0:T(1024)S(1)} %get-tuple-element.22), kind=kLoop, calls=%fused_computation.72 | loop fusion | flops 1373184 | bytes 28416 | tf_op jit(solution)/shard_map/reduce_or | solution.py:21
  1.9 1.0 %fusion.27 = s32[3072]{0:T(1024)S(1)} fusion(s32[64]{0:T(128)S(1)} %select_reduce_fusion.1, s32[64]{0:T(128)} %param.13, s32[3072]{0:T(1024)S(1)} %get-tuple-element.21, s32[64]{0:T(128)} %param.11, s32[64]{0:T(128)} %param.12, s32[3072]{0:T(1024)S(1)} %get-tuple-element.22), kind=kLoop, calls=%fused_computation.27 | loop fusion | flops 1766400 | bytes 37888 | tf_op jit(solution)/shard_map/reduce_sum | solution.py:23
  3.0 0.1 convert_element_type.89
  3.0 3.6 %fusion.8 = bf16[2048,32]{0,1:T(8,128)(2,1)S(1)} fusion(bf16[2048,1024]{1,0:T(8,128)(2,1)} %param.7, bf16[1024,16]{0,1:T(8,128)(2,1)} %param.10, bf16[1024,16]{0,1:T(8,128)(2,1)} %param.9), kind=kOutput, calls=%fused_computation.11 | convolution fusion | flops 134414336 | bytes 4390912 | tf_op jit(solution)/shard_map/dot_general | solution.py:86
  6.6 5.2 %fusion.19 = bf16[16,32,192]{2,1,0:T(8,128)(2,1)} fusion(f32[2048]{0:T(1024)S(1)} %iota_convert_fusion, f32[16,192]{1,0:T(8,128)S(1)} %convert_element_type.89, bf16[2048,32]{0,1:T(8,128)(2,1)S(1)} %fusion.8), kind=kOutput, calls=%fused_computation.20 | convolution fusion | flops 409042944 | bytes 348160 | tf_op jit(solution)/shard_map/jf,csj->cfs/dot_general | solution.py:88
  11.8 7.6 %all-to-all-start = ((bf16[16,32,192]{2,1,0:T(8,128)(2,1)}), bf16[16,32,192]{2,1,0:T(8,128)(2,1)S(1)}, u32[]{:S(2)}, u32[]{:S(2)}) async-start(bf16[16,32,192]{2,1,0:T(8,128)(2,1)} %fusion.19), calls=%async_computation | async-start | bytes 524288 | tf_op jit(solution)/shard_map/all_to_all | solution.py:95
  19.4 0.0 copy-done
  19.4 3.4 %convolution_convert_fusion = bf16[2048,256]{1,0:T(8,128)(2,1)S(1)} fusion(bf16[2048,1024]{1,0:T(8,128)(2,1)} %param.7, bf16[1024,256]{1,0:T(8,128)(2,1)S(1)} %copy-done), kind=kOutput, calls=%fused_computation.9 | convolution fusion | flops 1074266112 | bytes 5767168 | tf_op jit(solution)/shard_map/dot_general | solution.py:86
  22.9 0.0 copy-start.1
  22.9 0.0 copy-start.2
  22.9 0.0 copy-start.3
  22.9 4.8 %fusion.12 = bf16[16,256,192]{1,2,0:T(8,128)(2,1)} fusion(f32[2048]{0:T(1024)S(1)} %iota_convert_fusion, f32[16,192]{1,0:T(8,128)S(1)} %convert_element_type.89, bf16[2048,256]{1,0:T(8,128)(2,1)S(1)} %convolution_convert_fusion), kind=kOutput, calls=%fused_computation.13 | convolution fusion | flops 3228303360 | bytes 2641920 | tf_op jit(solution)/shard_map/jf,csj->cfs/dot_general | solution.py:88
  27.8 0.0 copy-done.1
  27.8 0.0 copy-done.2
  27.8 0.0 copy-done.3
  27.8 0.1 fusion.69
  27.9 0.1 select_reduce_fusion
  28.0 0.0 all-to-all-done
  28.0 6.7 %all-to-all-start.1 = ((bf16[16,256,192]{1,2,0:T(8,128)(2,1)}), bf16[16,256,192]{1,2,0:T(8,128)(2,1)S(1)}, u32[]{:S(2)}, u32[]{:S(2)}) async-start(bf16[16,256,192]{1,2,0:T(8,128)(2,1)} %fusion.12), calls=%async_computation.1 | async-start | bytes 3145728 | tf_op jit(solution)/shard_map/all_to_all | solution.py:96
  34.7 0.1 compare_and_fusion
  34.9 0.4 multiply_cosine_fusion
  35.3 0.1 convert_reduce_fusion.1
  35.3 24.4 %all-gather.1 = bf16[8,192,32]{1,2,0:T(8,128)(2,1)S(1)} all-gather(bf16[1,192,32]{1,2,0:T(8,128)(2,1)S(1)} %bitcast.71), channel_id=2, replica_groups={{0,1,2,3,4,5,6,7},{8,9,10,11,12,13,14,15},{16,17,18,19,20,21,22,23},{24..., dimensions={0}, use_global_device_ids=true | all-gather | bytes 110592 | tf_op jit(solution)/shard_map/all_gather | solution.py:98
  59.8 0.1 copy.33
  59.9 0.1 copy.34
  60.0 0.4 fusion.54
  60.4 0.0 all-to-all-done.1
  60.4 0.2 convert_reduce_fusion
  60.7 0.1 reshape.307
  60.8 0.3 fusion.70
  61.0 0.1 subtract_convert_fusion
  61.1 0.3 fusion.72
  61.4 0.1 fusion.30
  61.5 0.3 fusion.24
  61.8 0.1 copy.29
  61.9 0.7 %copy.43 = bf16[24,8,2,128]{3,1,2,0:T(8,128)(2,1)} copy(bf16[24,8,2,128]{3,2,1,0:T(2,128)(2,1)S(1)} %bitcast.69) | data formatting | bytes 196608
  (9 shorter events, 0.1 us)
Async XLA Ops:
  0.0 19.4 %copy-start = (bf16[1024,256]{1,0:T(8,128)(2,1)S(1)}, bf16[1024,256]{1,0:T(8,128)(2,1)}, u32[]{:S(2)}) copy-start(bf16[1024,256]{1,0:T(8,128)(2,1)} %param.8) | copy-start | bytes 1572868
  11.8 16.2 %all-to-all-start = ((bf16[16,32,192]{2,1,0:T(8,128)(2,1)}), bf16[16,32,192]{2,1,0:T(8,128)(2,1)S(1)}, u32[]{:S(2)}, u32[]{:S(2)}) async-start(bf16[16,32,192]{2,1,0:T(8,128)(2,1)} %fusion.19), calls=%async_computation | async-start | bytes 524288 | tf_op jit(solution)/shard_map/all_to_all | solution.py:95
  22.9 4.9 %copy-start.1 = (s32[64]{0:T(128)S(1)}, s32[64]{0:T(128)}, u32[]{:S(2)}) copy-start(s32[64]{0:T(128)} %param.11) | copy-start | bytes 772
  22.9 4.9 %copy-start.2 = (s32[64]{0:T(128)S(1)}, s32[64]{0:T(128)}, u32[]{:S(2)}) copy-start(s32[64]{0:T(128)} %param.13) | copy-start | bytes 772
  22.9 4.9 %copy-start.3 = (s32[64]{0:T(128)S(1)}, s32[64]{0:T(128)}, u32[]{:S(2)}) copy-start(s32[64]{0:T(128)} %param.12) | copy-start | bytes 772
  28.0 32.4 %all-to-all-start.1 = ((bf16[16,256,192]{1,2,0:T(8,128)(2,1)}), bf16[16,256,192]{1,2,0:T(8,128)(2,1)S(1)}, u32[]{:S(2)}, u32[]{:S(2)}) async-start(bf16[16,256,192]{1,2,0:T(8,128)(2,1)} %fusion.12), calls=%async_computation.1 | async-start | bytes 3145728 | tf_op jit(solution)/shard_map/all_to_all | solution.py:96

commit v10 on v9

--- a/solution.py
+++ b/solution.py
@@ -20,7 +20,7 @@
     )
     filled = jnp.any(match, axis=1)
     position = jnp.sum(jnp.where(match, offset, 0), axis=1)
-    source = jnp.sum(jnp.where(match, starts[None, :] + offset, 0), axis=1)
+    source = jnp.sum(jnp.where(match, starts[None, :] + offset + 1, 0), axis=1) - 1
     doc_of = jnp.sum(jnp.where(match, doc_ids[None, :], 0), axis=1)
     slot_doc = jnp.where(filled, doc_of, -1 - slot_ids)
     return (source, filled, slot_doc, position)
@@ -72,11 +72,10 @@
         for g in range(lax.axis_size("tp") // members)
     ]
 
-    source, filled, _, _ = slot_table(
+    source, _, _, _ = slot_table(
         jnp.arange(slot_total, dtype=jnp.int32), doc_len, doc_shard, doc_slot, capacity
     )
     token_ids = jnp.arange(total_tokens, dtype=jnp.int32)
-    source = jnp.where(filled, source, -1)
     placement = (
         source.astype(jnp.float32)[:, None] == token_ids.astype(jnp.float32)[None, :]
     ).astype(jnp.bfloat16)

time: 62.9 us -> 61.9 us (0.984)
  other arithmetic: 4.59 us -> 3.55 us
    reduce_or x2 -> x1, other arithmetic: 1.18 us -> 0.11 us  [slot_table(): filled = jnp.any(match, axis=1)]
where the time goes in v10:
time: 61.9 us; the launch traced here: 61.5 us
  blocking collectives  24.4 us (39%)
  matrix products  17.7 us (29%)
  starting transfers between devices  14.2 us (23%)
  other arithmetic  3.55 us (6%)
  local copies, waits for them, and re-layouts  1.42 us (2%)
    all_gather x1, blocking collectives, body(): lax.all_gather(jnp.transpose(kv_summed).astype(jnp.bfloat16), 'tp', axis=...  24.4 us
    dot_general x2, matrix products, placed(): jnp.einsum('jf,csj->cfs', term, placement.reshape(shards, capacity, total...  10.1 us
    all_to_all x1, starting transfers between devices, body(): lax.all_to_all(placed(jnp.concatenate([wk, wv], axis=1)), 'ctx', 0, 0, ti...  7.58 us
    dot_general x2, matrix products, placed(): jnp.dot(tokens, weights, preferred_element_type=jnp.float32)  6.99 us
    all_to_all x1, starting transfers between devices, body(): q_received = lax.all_to_all(placed(wq), 'ctx', 0, 0, tiled=False)  6.66 us
  transfers between devices with their start and end apart: 2, of which 0 were waited for; matrix products, arithmetic and copies ran while one was open for 16% of the time, Pallas kernels for 0%

profile of v10, /device:TPU:1, one launch (start us, length us, event | category | flops | bytes accessed | tf_op | source)
XLA Modules:
  0.0 61.5 jit_solution(9196929103509275371)
XLA Ops:
  0.0 0.0 copy-start
  0.0 0.8 %select_reduce_fusion.1 = s32[64]{0:T(128)S(1)} fusion(s32[64]{0:T(128)} %param.11), kind=kLoop, calls=%fused_computation.73 | loop fusion | flops 12224 | bytes 512 | tf_op jit(solution)/shard_map/reduce_sum | solution.py:14
  0.8 1.0 %fusion.28 = s32[3072]{0:T(1024)S(1)} fusion(s32[64]{0:T(128)S(1)} %select_reduce_fusion.1, s32[64]{0:T(128)} %param.11, s32[64]{0:T(128)} %param.13, s32[3072]{0:T(1024)S(1)} %get-tuple-element.21, s32[3072]{0:T(1024)S(1)} %get-tuple-element.22, s32[64]{0:T(128)} %param.12), kind=kLoop, calls=%fused_computation.28 | loop fusion | flops 1963008 | bytes 37888 | tf_op jit(solution)/shard_map/reduce_sum | solution.py:23
  1.9 0.1 convert_element_type.89
  2.0 3.6 %fusion.8 = bf16[2048,32]{0,1:T(8,128)(2,1)S(1)} fusion(bf16[2048,1024]{1,0:T(8,128)(2,1)} %param.7, bf16[1024,16]{0,1:T(8,128)(2,1)} %param.10, bf16[1024,16]{0,1:T(8,128)(2,1)} %param.9), kind=kOutput, calls=%fused_computation.11 | convolution fusion | flops 134414336 | bytes 4390912 | tf_op jit(solution)/shard_map/dot_general | solution.py:85
  5.5 5.2 %fusion.19 = bf16[16,32,192]{2,1,0:T(8,128)(2,1)} fusion(f32[2048]{0:T(1024)S(1)} %iota_convert_fusion, f32[16,192]{1,0:T(8,128)S(1)} %convert_element_type.89, bf16[2048,32]{0,1:T(8,128)(2,1)S(1)} %fusion.8), kind=kOutput, calls=%fused_computation.20 | convolution fusion | flops 409042944 | bytes 348160 | tf_op jit(solution)/shard_map/jf,csj->cfs/dot_general | solution.py:87
  10.8 7.6 %all-to-all-start = ((bf16[16,32,192]{2,1,0:T(8,128)(2,1)}), bf16[16,32,192]{2,1,0:T(8,128)(2,1)S(1)}, u32[]{:S(2)}, u32[]{:S(2)}) async-start(bf16[16,32,192]{2,1,0:T(8,128)(2,1)} %fusion.19), calls=%async_computation | async-start | bytes 524288 | tf_op jit(solution)/shard_map/all_to_all | solution.py:94
  18.4 0.0 copy-done
  18.4 3.4 %convolution_convert_fusion = bf16[2048,256]{1,0:T(8,128)(2,1)S(1)} fusion(bf16[2048,1024]{1,0:T(8,128)(2,1)} %param.7, bf16[1024,256]{1,0:T(8,128)(2,1)S(1)} %copy-done), kind=kOutput, calls=%fused_computation.9 | convolution fusion | flops 1074266112 | bytes 5767168 | tf_op jit(solution)/shard_map/dot_general | solution.py:85
  21.8 0.0 copy-start.1
  21.8 0.0 copy-start.2
  21.9 0.0 copy-start.3
  21.9 4.8 %fusion.12 = bf16[16,256,192]{1,2,0:T(8,128)(2,1)} fusion(f32[2048]{0:T(1024)S(1)} %iota_convert_fusion, f32[16,192]{1,0:T(8,128)S(1)} %convert_element_type.89, bf16[2048,256]{1,0:T(8,128)(2,1)S(1)} %convolution_convert_fusion), kind=kOutput, calls=%fused_computation.13 | convolution fusion | flops 3228303360 | bytes 2641920 | tf_op jit(solution)/shard_map/jf,csj->cfs/dot_general | solution.py:87
  26.7 0.0 copy-done.1
  26.7 0.0 copy-done.2
  26.7 0.0 copy-done.3
  26.8 0.1 fusion.69
  26.9 0.1 select_reduce_fusion
  27.0 0.0 all-to-all-done
  27.0 6.7 %all-to-all-start.1 = ((bf16[16,256,192]{1,2,0:T(8,128)(2,1)}), bf16[16,256,192]{1,2,0:T(8,128)(2,1)S(1)}, u32[]{:S(2)}, u32[]{:S(2)}) async-start(bf16[16,256,192]{1,2,0:T(8,128)(2,1)} %fusion.12), calls=%async_computation.1 | async-start | bytes 3145728 | tf_op jit(solution)/shard_map/all_to_all | solution.py:95
  33.7 0.1 compare_and_fusion
  33.8 0.4 multiply_cosine_fusion
  34.2 0.1 convert_reduce_fusion.1
  34.3 24.4 %all-gather.1 = bf16[8,192,32]{1,2,0:T(8,128)(2,1)S(1)} all-gather(bf16[1,192,32]{1,2,0:T(8,128)(2,1)S(1)} %bitcast.71), channel_id=2, replica_groups={{0,1,2,3,4,5,6,7},{8,9,10,11,12,13,14,15},{16,17,18,19,20,21,22,23},{24..., dimensions={0}, use_global_device_ids=true | all-gather | bytes 110592 | tf_op jit(solution)/shard_map/all_gather | solution.py:97
  58.7 0.1 copy.34
  58.8 0.1 copy.33
  58.9 0.4 fusion.55
  59.4 0.0 all-to-all-done.1
  59.4 0.2 convert_reduce_fusion
  59.6 0.1 reshape.304
  59.7 0.3 fusion.70
  60.0 0.1 subtract_convert_fusion
  60.1 0.3 fusion.72
  60.4 0.1 fusion.31
  60.5 0.3 fusion.24
  60.8 0.1 copy.29
  60.9 0.7 %copy.43 = bf16[24,8,2,128]{3,1,2,0:T(8,128)(2,1)} copy(bf16[24,8,2,128]{3,2,1,0:T(2,128)(2,1)S(1)} %bitcast.69) | data formatting | bytes 196608
  (9 shorter events, 0.1 us)
Async XLA Ops:
  0.0 18.4 %copy-start = (bf16[1024,256]{1,0:T(8,128)(2,1)S(1)}, bf16[1024,256]{1,0:T(8,128)(2,1)}, u32[]{:S(2)}) copy-start(bf16[1024,256]{1,0:T(8,128)(2,1)} %param.8) | copy-start | bytes 1572868
  10.8 16.2 %all-to-all-start = ((bf16[16,32,192]{2,1,0:T(8,128)(2,1)}), bf16[16,32,192]{2,1,0:T(8,128)(2,1)S(1)}, u32[]{:S(2)}, u32[]{:S(2)}) async-start(bf16[16,32,192]{2,1,0:T(8,128)(2,1)} %fusion.19), calls=%async_computation | async-start | bytes 524288 | tf_op jit(solution)/shard_map/all_to_all | solution.py:94
  21.8 4.9 %copy-start.1 = (s32[64]{0:T(128)S(1)}, s32[64]{0:T(128)}, u32[]{:S(2)}) copy-start(s32[64]{0:T(128)} %param.11) | copy-start | bytes 772
  21.8 4.9 %copy-start.2 = (s32[64]{0:T(128)S(1)}, s32[64]{0:T(128)}, u32[]{:S(2)}) copy-start(s32[64]{0:T(128)} %param.13) | copy-start | bytes 772
  21.9 4.9 %copy-start.3 = (s32[64]{0:T(128)S(1)}, s32[64]{0:T(128)}, u32[]{:S(2)}) copy-start(s32[64]{0:T(128)} %param.12) | copy-start | bytes 772
  27.0 32.4 %all-to-all-start.1 = ((bf16[16,256,192]{1,2,0:T(8,128)(2,1)}), bf16[16,256,192]{1,2,0:T(8,128)(2,1)S(1)}, u32[]{:S(2)}, u32[]{:S(2)}) async-start(bf16[16,256,192]{1,2,0:T(8,128)(2,1)} %fusion.12), calls=%async_computation.1 | async-start | bytes 3145728 | tf_op jit(solution)/shard_map/all_to_all | solution.py:95

commit v11 on v10

--- a/solution.py
+++ b/solution.py
@@ -41,20 +41,23 @@
 
 
 def attend(query_matrix, key, value_matrix, slot_doc, slot_position_index):
+    heads = query_matrix.shape[1]
     scale = query_matrix.shape[-1] ** (-0.5)
-    scores = (
-        jnp.einsum("qgjd,kgd->gjqk", query_matrix, key, preferred_element_type=jnp.float32) * scale
-    )
+    scores = jnp.einsum("qjd,kd->qjk", query_matrix, key, preferred_element_type=jnp.float32) * scale
     allowed = (slot_doc[:, None] == slot_doc[None, :]) & (
         slot_position_index[None, :] <= slot_position_index[:, None]
     )
-    scores = jnp.where(allowed[None, None], scores, -jnp.inf)
+    scores = jnp.where(allowed[:, None, :], scores, -jnp.inf)
     peak = jnp.max(scores, axis=-1, keepdims=True)
     expo = jnp.exp(scores - peak)
     total = jnp.sum(expo, axis=-1)
-    weights = expo.astype(jnp.bfloat16)
-    mixed = jnp.einsum("gjqk,kgd->qgjd", weights, value_matrix, preferred_element_type=jnp.float32)
-    result = mixed / jnp.transpose(total, (2, 0, 1))[..., None]
+    weights = expo.astype(jnp.bfloat16).reshape(expo.shape[0], -1)
+    diagonal = jnp.eye(heads, dtype=value_matrix.dtype)
+    spread = (diagonal[:, None, :, None] * value_matrix[None, :, None, :]).reshape(
+        heads * value_matrix.shape[0], heads * value_matrix.shape[1]
+    )
+    mixed = jnp.dot(weights, spread, preferred_element_type=jnp.float32)
+    result = mixed / jnp.repeat(total, value_matrix.shape[1], axis=1)
     return result.astype(jnp.bfloat16)
 
 
@@ -109,14 +112,13 @@
         q_summed.reshape(capacity, heads_here, HEAD_SIZE), my_pos
     ).astype(jnp.bfloat16)
     key = apply_rotary(key_unrotated.astype(jnp.float32)[:, None, :], my_pos).astype(jnp.bfloat16)
-    result = attend(
-        query_matrix.reshape(capacity, 1, heads_here, HEAD_SIZE),
-        key,
-        value_matrix[:, None, :],
+    return attend(
+        query_matrix,
+        key.reshape(capacity, HEAD_SIZE),
+        value_matrix,
         my_doc,
         my_pos,
     )
-    return result.reshape(capacity, heads_here * HEAD_SIZE)
 
 
 def solution(mesh):

time: 61.9 us -> 62.4 us (level)
  matrix products: 17.7 us -> 18.4 us
    unnamed x11 -> x10, local copies, waits for them, and re-layouts: 0.86 us -> 0.22 us
where the time goes in v11:
time: 62.4 us; the launch traced here: 62.1 us
  blocking collectives  24.4 us (39%)
  matrix products  18.4 us (29%)
  starting transfers between devices  14.2 us (23%)
  other arithmetic  3.68 us (6%)
  local copies, waits for them, and re-layouts  1.18 us (2%)
    all_gather x1, blocking collectives, body(): lax.all_gather(jnp.transpose(kv_summed).astype(jnp.bfloat16), 'tp', axis=...  24.4 us
    dot_general x2, matrix products, placed(): jnp.einsum('jf,csj->cfs', term, placement.reshape(shards, capacity, total...  10.1 us
    all_to_all x1, starting transfers between devices, body(): lax.all_to_all(placed(jnp.concatenate([wk, wv], axis=1)), 'ctx', 0, 0, ti...  7.59 us
    dot_general x2, matrix products, placed(): jnp.dot(tokens, weights, preferred_element_type=jnp.float32)  6.99 us
    all_to_all x1, starting transfers between devices, body(): q_received = lax.all_to_all(placed(wq), 'ctx', 0, 0, tiled=False)  6.66 us
  transfers between devices with their start and end apart: 2, of which 0 were waited for; matrix products, arithmetic and copies ran while one was open for 16% of the time, Pallas kernels for 0%

profile of v11, /device:TPU:1, one launch (start us, length us, event | category | flops | bytes accessed | tf_op | source)
XLA Modules:
  0.0 62.1 jit_solution(4378654012511810853)
XLA Ops:
  0.0 0.0 copy-start
  0.0 0.8 %select_reduce_fusion.1 = s32[64]{0:T(128)S(1)} fusion(s32[64]{0:T(128)} %param.11), kind=kLoop, calls=%fused_computation.71 | loop fusion | flops 12224 | bytes 512 | tf_op jit(solution)/shard_map/reduce_sum | solution.py:14
  0.8 1.0 %fusion.29 = s32[3072]{0:T(1024)S(1)} fusion(s32[64]{0:T(128)S(1)} %select_reduce_fusion.1, s32[64]{0:T(128)} %param.11, s32[64]{0:T(128)} %param.13, s32[3072]{0:T(1024)S(1)} %get-tuple-element.24, s32[3072]{0:T(1024)S(1)} %get-tuple-element.25, s32[64]{0:T(128)} %param.12), kind=kLoop, calls=%fused_computation.29 | loop fusion | flops 1963008 | bytes 37888 | tf_op jit(solution)/shard_map/reduce_sum | solution.py:23
  1.9 0.1 convert_element_type.94
  2.0 3.6 %fusion.9 = bf16[2048,32]{0,1:T(8,128)(2,1)S(1)} fusion(bf16[2048,1024]{1,0:T(8,128)(2,1)} %param.7, bf16[1024,16]{0,1:T(8,128)(2,1)} %param.10, bf16[1024,16]{0,1:T(8,128)(2,1)} %param.9), kind=kOutput, calls=%fused_computation.12 | convolution fusion | flops 134414336 | bytes 4390912 | tf_op jit(solution)/shard_map/dot_general | solution.py:88
  5.5 0.0 copy-start.1
  5.6 0.0 copy-start.2
  5.6 0.0 copy-start.3
  5.6 5.2 %fusion.22 = bf16[16,32,192]{2,1,0:T(8,128)(2,1)} fusion(f32[2048]{0:T(1024)S(1)} %iota_convert_fusion, f32[16,192]{1,0:T(8,128)S(1)} %convert_element_type.94, bf16[2048,32]{0,1:T(8,128)(2,1)S(1)} %fusion.9), kind=kOutput, calls=%fused_computation.23 | convolution fusion | flops 409042944 | bytes 348160 | tf_op jit(solution)/shard_map/jf,csj->cfs/dot_general | solution.py:90
  10.8 7.6 %all-to-all-start.1 = ((bf16[16,32,192]{2,1,0:T(8,128)(2,1)}), bf16[16,32,192]{2,1,0:T(8,128)(2,1)S(1)}, u32[]{:S(2)}, u32[]{:S(2)}) async-start(bf16[16,32,192]{2,1,0:T(8,128)(2,1)} %fusion.22), calls=%async_computation.1 | async-start | bytes 524288 | tf_op jit(solution)/shard_map/all_to_all | solution.py:97
  18.4 0.0 copy-done.1
  18.4 0.0 copy-done.2
  18.4 0.0 copy-done.3
  18.5 0.1 select_reduce_fusion
  18.6 0.1 fusion.76
  18.7 0.0 copy-done
  18.7 3.4 %convolution_convert_fusion = bf16[2048,256]{1,0:T(8,128)(2,1)S(1)} fusion(bf16[2048,1024]{1,0:T(8,128)(2,1)} %param.7, bf16[1024,256]{1,0:T(8,128)(2,1)S(1)} %copy-done), kind=kOutput, calls=%fused_computation.10 | convolution fusion | flops 1074266112 | bytes 5767168 | tf_op jit(solution)/shard_map/dot_general | solution.py:88
  22.1 4.8 %fusion.13 = bf16[16,256,192]{1,2,0:T(8,128)(2,1)} fusion(f32[2048]{0:T(1024)S(1)} %iota_convert_fusion, f32[16,192]{1,0:T(8,128)S(1)} %convert_element_type.94, bf16[2048,256]{1,0:T(8,128)(2,1)S(1)} %convolution_convert_fusion), kind=kOutput, calls=%fused_computation.14 | convolution fusion | flops 3228303360 | bytes 2641920 | tf_op jit(solution)/shard_map/jf,csj->cfs/dot_general | solution.py:90
  27.0 0.1 compare_and_fusion
  27.1 0.0 all-to-all-done.1
  27.1 6.7 %all-to-all-start = ((bf16[16,256,192]{1,2,0:T(8,128)(2,1)}), bf16[16,256,192]{1,2,0:T(8,128)(2,1)S(1)}, u32[]{:S(2)}, u32[]{:S(2)}) async-start(bf16[16,256,192]{1,2,0:T(8,128)(2,1)} %fusion.13), calls=%async_computation | async-start | bytes 3145728 | tf_op jit(solution)/shard_map/all_to_all | solution.py:98
  33.8 0.4 multiply_cosine_fusion.1
  34.2 0.1 convert_reduce_fusion.1
  34.3 24.4 %all-gather.1 = bf16[8,192,32]{1,2,0:T(8,128)(2,1)S(1)} all-gather(bf16[1,192,32]{1,2,0:T(8,128)(2,1)S(1)} %bitcast.55), channel_id=2, replica_groups={{0,1,2,3,4,5,6,7},{8,9,10,11,12,13,14,15},{16,17,18,19,20,21,22,23},{24..., dimensions={0}, use_global_device_ids=true | all-gather | bytes 110592 | tf_op jit(solution)/shard_map/all_gather | solution.py:100
  58.7 0.1 copy.28
  58.8 0.1 copy.27
  58.9 0.1 copy.23
  59.0 0.2 broadcast_multiply_fusion
  59.3 0.4 fusion.53
  59.7 0.0 all-to-all-done
  59.7 0.2 convert_reduce_fusion
  59.9 0.1 reshape.291
  60.0 0.3 fusion.78
  60.3 0.1 subtract_convert_fusion
  60.4 0.4 fusion.77
  60.8 0.1 copy.24
  60.9 0.3 broadcast_in_dim.41
  61.2 0.9 %fusion.25 = bf16[192,256]{1,0:T(8,128)(2,1)} fusion(bf16[192,384]{0,1:T(8,128)(2,1)S(1)} %bitcast.56, f32[24,8,2,128]{3,2,1,0:T(2,128)S(1)} %bitcast.53, bf16[48,8,2,128]{3,2,1,0:T(2,128)(2,1)S(1)} %bitcast.54), kind=kOutput, calls=%fused_computation.25 | convolution fusion | flops 37847040 | bytes 638976 | tf_op jit(solution)/shard_map/dot_general | solution.py:59
  (10 shorter events, 0.1 us)
Async XLA Ops:
  0.0 18.7 %copy-start = (bf16[1024,256]{1,0:T(8,128)(2,1)S(1)}, bf16[1024,256]{1,0:T(8,128)(2,1)}, u32[]{:S(2)}) copy-start(bf16[1024,256]{1,0:T(8,128)(2,1)} %param.8) | copy-start | bytes 1572868
  5.5 12.9 %copy-start.1 = (s32[64]{0:T(128)S(1)}, s32[64]{0:T(128)}, u32[]{:S(2)}) copy-start(s32[64]{0:T(128)} %param.11) | copy-start | bytes 772
  5.6 12.9 %copy-start.2 = (s32[64]{0:T(128)S(1)}, s32[64]{0:T(128)}, u32[]{:S(2)}) copy-start(s32[64]{0:T(128)} %param.13) | copy-start | bytes 772
  5.6 12.9 %copy-start.3 = (s32[64]{0:T(128)S(1)}, s32[64]{0:T(128)}, u32[]{:S(2)}) copy-start(s32[64]{0:T(128)} %param.12) | copy-start | bytes 772
  10.8 16.3 %all-to-all-start.1 = ((bf16[16,32,192]{2,1,0:T(8,128)(2,1)}), bf16[16,32,192]{2,1,0:T(8,128)(2,1)S(1)}, u32[]{:S(2)}, u32[]{:S(2)}) async-start(bf16[16,32,192]{2,1,0:T(8,128)(2,1)} %fusion.22), calls=%async_computation.1 | async-start | bytes 524288 | tf_op jit(solution)/shard_map/all_to_all | solution.py:97
  27.1 32.6 %all-to-all-start = ((bf16[16,256,192]{1,2,0:T(8,128)(2,1)}), bf16[16,256,192]{1,2,0:T(8,128)(2,1)S(1)}, u32[]{:S(2)}, u32[]{:S(2)}) async-start(bf16[16,256,192]{1,2,0:T(8,128)(2,1)} %fusion.13), calls=%async_computation | async-start | bytes 3145728 | tf_op jit(solution)/shard_map/all_to_all | solution.py:98

commit v12 on v11

--- a/solution.py
+++ b/solution.py
@@ -11,7 +11,11 @@
 
 def slot_table(slot_ids, doc_len, doc_shard, doc_slot, capacity):
     doc_ids = jnp.arange(doc_len.shape[0], dtype=jnp.int32)
-    starts = jnp.sum(jnp.where(doc_ids[None, :] < doc_ids[:, None], doc_len[None, :], 0), axis=1)
+    starts = jnp.dot(
+        (doc_ids[None, :] < doc_ids[:, None]).astype(jnp.float32),
+        doc_len.astype(jnp.float32),
+        precision=lax.Precision.HIGHEST,
+    ).astype(jnp.int32)
     shard_of = slot_ids // capacity
     local = slot_ids % capacity
     offset = local[:, None] - doc_slot[None, :]

time: 62.4 us -> 62.5 us (level)
  matrix products: 18.4 us -> 19.2 us
  other arithmetic: 3.68 us -> 2.9 us
    dot_general x0 -> x1, matrix products: none -> 0.83 us  [slot_table(): jnp.dot((doc_ids[None, :] < doc_ids[:, None]).astype(jnp.float32), doc_le...]
    reduce_sum x1 -> x0, other arithmetic: 0.82 us -> none  [slot_table(): jnp.sum(jnp.where(doc_ids[None, :] < doc_ids[:, None], doc_len[None, :],...]
where the time goes in v12:
time: 62.5 us; the launch traced here: 62.1 us
  blocking collectives  24.4 us (39%)
  matrix products  19.2 us (31%)
  starting transfers between devices  14.2 us (23%)
  other arithmetic  2.9 us (5%)
  local copies, waits for them, and re-layouts  1.18 us (2%)
    all_gather x1, blocking collectives, body(): lax.all_gather(jnp.transpose(kv_summed).astype(jnp.bfloat16), 'tp', axis=...  24.4 us
    dot_general x2, matrix products, placed(): jnp.einsum('jf,csj->cfs', term, placement.reshape(shards, capacity, total...  10.1 us
    all_to_all x1, starting transfers between devices, body(): lax.all_to_all(placed(jnp.concatenate([wk, wv], axis=1)), 'ctx', 0, 0, ti...  7.59 us
    dot_general x2, matrix products, placed(): jnp.dot(tokens, weights, preferred_element_type=jnp.float32)  6.99 us
    all_to_all x1, starting transfers between devices, body(): q_received = lax.all_to_all(placed(wq), 'ctx', 0, 0, tiled=False)  6.66 us
  transfers between devices with their start and end apart: 2, of which 0 were waited for; matrix products, arithmetic and copies ran while one was open for 16% of the time, Pallas kernels for 0%

profile of v12, /device:TPU:1, one launch (start us, length us, event | category | flops | bytes accessed | tf_op | source)
XLA Modules:
  0.0 62.1 jit_solution(986893095972577127)
XLA Ops:
  0.0 0.0 copy-start
  0.0 0.8 %fusion.26 = s32[64]{0:T(128)S(1)} fusion(s32[64]{0:T(128)} %param.11), kind=kOutput, calls=%fused_computation.27 | convolution fusion | flops 53376 | bytes 512 | tf_op jit(solution)/shard_map/dot_general | solution.py:14
  0.9 1.1 %fusion.30 = s32[3072]{0:T(1024)S(1)} fusion(s32[64]{0:T(128)S(1)} %fusion.26, s32[64]{0:T(128)} %param.11, s32[64]{0:T(128)} %param.13, s32[3072]{0:T(1024)S(1)} %get-tuple-element.24, s32[3072]{0:T(1024)S(1)} %get-tuple-element.25, s32[64]{0:T(128)} %param.12), kind=kLoop, calls=%fused_computation.31 | loop fusion | flops 1963008 | bytes 37888 | tf_op jit(solution)/shard_map/reduce_sum | solution.py:27
  1.9 0.1 convert_element_type.103
  2.0 3.6 %fusion.9 = bf16[2048,32]{0,1:T(8,128)(2,1)S(1)} fusion(bf16[2048,1024]{1,0:T(8,128)(2,1)} %param.7, bf16[1024,16]{0,1:T(8,128)(2,1)} %param.10, bf16[1024,16]{0,1:T(8,128)(2,1)} %param.9), kind=kOutput, calls=%fused_computation.12 | convolution fusion | flops 134414336 | bytes 4390912 | tf_op jit(solution)/shard_map/dot_general | solution.py:92
  5.6 0.0 copy-start.1
  5.6 0.0 copy-start.2
  5.6 0.0 copy-start.3
  5.6 5.2 %fusion.22 = bf16[16,32,192]{2,1,0:T(8,128)(2,1)} fusion(f32[2048]{0:T(1024)S(1)} %iota_convert_fusion, f32[16,192]{1,0:T(8,128)S(1)} %convert_element_type.103, bf16[2048,32]{0,1:T(8,128)(2,1)S(1)} %fusion.9), kind=kOutput, calls=%fused_computation.23 | convolution fusion | flops 409042944 | bytes 348160 | tf_op jit(solution)/shard_map/jf,csj->cfs/dot_general | solution.py:94
  10.8 7.6 %all-to-all-start.1 = ((bf16[16,32,192]{2,1,0:T(8,128)(2,1)}), bf16[16,32,192]{2,1,0:T(8,128)(2,1)S(1)}, u32[]{:S(2)}, u32[]{:S(2)}) async-start(bf16[16,32,192]{2,1,0:T(8,128)(2,1)} %fusion.22), calls=%async_computation.1 | async-start | bytes 524288 | tf_op jit(solution)/shard_map/all_to_all | solution.py:101
  18.5 0.0 copy-done.1
  18.5 0.0 copy-done.2
  18.5 0.0 copy-done.3
  18.5 0.1 select_reduce_fusion
  18.6 0.1 fusion.77
  18.7 0.0 copy-done
  18.7 3.4 %convolution_convert_fusion = bf16[2048,256]{1,0:T(8,128)(2,1)S(1)} fusion(bf16[2048,1024]{1,0:T(8,128)(2,1)} %param.7, bf16[1024,256]{1,0:T(8,128)(2,1)S(1)} %copy-done), kind=kOutput, calls=%fused_computation.10 | convolution fusion | flops 1074266112 | bytes 5767168 | tf_op jit(solution)/shard_map/dot_general | solution.py:92
  22.2 4.8 %fusion.13 = bf16[16,256,192]{1,2,0:T(8,128)(2,1)} fusion(f32[2048]{0:T(1024)S(1)} %iota_convert_fusion, f32[16,192]{1,0:T(8,128)S(1)} %convert_element_type.103, bf16[2048,256]{1,0:T(8,128)(2,1)S(1)} %convolution_convert_fusion), kind=kOutput, calls=%fused_computation.14 | convolution fusion | flops 3228303360 | bytes 2641920 | tf_op jit(solution)/shard_map/jf,csj->cfs/dot_general | solution.py:94
  27.0 0.1 compare_and_fusion
  27.1 0.0 all-to-all-done.1
  27.2 6.7 %all-to-all-start = ((bf16[16,256,192]{1,2,0:T(8,128)(2,1)}), bf16[16,256,192]{1,2,0:T(8,128)(2,1)S(1)}, u32[]{:S(2)}, u32[]{:S(2)}) async-start(bf16[16,256,192]{1,2,0:T(8,128)(2,1)} %fusion.13), calls=%async_computation | async-start | bytes 3145728 | tf_op jit(solution)/shard_map/all_to_all | solution.py:102
  33.9 0.4 multiply_cosine_fusion.1
  34.3 0.1 convert_reduce_fusion.1
  34.3 24.4 %all-gather.1 = bf16[8,192,32]{1,2,0:T(8,128)(2,1)S(1)} all-gather(bf16[1,192,32]{1,2,0:T(8,128)(2,1)S(1)} %bitcast.62), channel_id=2, replica_groups={{0,1,2,3,4,5,6,7},{8,9,10,11,12,13,14,15},{16,17,18,19,20,21,22,23},{24..., dimensions={0}, use_global_device_ids=true | all-gather | bytes 110592 | tf_op jit(solution)/shard_map/all_gather | solution.py:104
  58.8 0.1 copy.28
  58.9 0.1 copy.27
  59.0 0.1 copy.23
  59.1 0.2 broadcast_multiply_fusion
  59.3 0.4 fusion.54
  59.7 0.0 all-to-all-done
  59.8 0.2 convert_reduce_fusion
  60.0 0.1 reshape.291
  60.1 0.3 fusion.79
  60.4 0.1 subtract_convert_fusion
  60.4 0.4 fusion.78
  60.8 0.1 copy.24
  61.0 0.3 broadcast_in_dim.23
  61.2 0.9 %fusion.25 = bf16[192,256]{1,0:T(8,128)(2,1)} fusion(bf16[192,384]{0,1:T(8,128)(2,1)S(1)} %bitcast.63, f32[24,8,2,128]{3,2,1,0:T(2,128)S(1)} %bitcast.60, bf16[48,8,2,128]{3,2,1,0:T(2,128)(2,1)S(1)} %bitcast.61), kind=kOutput, calls=%fused_computation.25 | convolution fusion | flops 37847040 | bytes 638976 | tf_op jit(solution)/shard_map/dot_general | solution.py:63
  (10 shorter events, 0.1 us)
Async XLA Ops:
  0.0 18.7 %copy-start = (bf16[1024,256]{1,0:T(8,128)(2,1)S(1)}, bf16[1024,256]{1,0:T(8,128)(2,1)}, u32[]{:S(2)}) copy-start(bf16[1024,256]{1,0:T(8,128)(2,1)} %param.8) | copy-start | bytes 1572868
  5.6 12.9 %copy-start.1 = (s32[64]{0:T(128)S(1)}, s32[64]{0:T(128)}, u32[]{:S(2)}) copy-start(s32[64]{0:T(128)} %param.11) | copy-start | bytes 772
  5.6 12.9 %copy-start.2 = (s32[64]{0:T(128)S(1)}, s32[64]{0:T(128)}, u32[]{:S(2)}) copy-start(s32[64]{0:T(128)} %param.13) | copy-start | bytes 772
  5.6 12.9 %copy-start.3 = (s32[64]{0:T(128)S(1)}, s32[64]{0:T(128)}, u32[]{:S(2)}) copy-start(s32[64]{0:T(128)} %param.12) | copy-start | bytes 772
  10.8 16.3 %all-to-all-start.1 = ((bf16[16,32,192]{2,1,0:T(8,128)(2,1)}), bf16[16,32,192]{2,1,0:T(8,128)(2,1)S(1)}, u32[]{:S(2)}, u32[]{:S(2)}) async-start(bf16[16,32,192]{2,1,0:T(8,128)(2,1)} %fusion.22), calls=%async_computation.1 | async-start | bytes 524288 | tf_op jit(solution)/shard_map/all_to_all | solution.py:101
  27.2 32.6 %all-to-all-start = ((bf16[16,256,192]{1,2,0:T(8,128)(2,1)}), bf16[16,256,192]{1,2,0:T(8,128)(2,1)S(1)}, u32[]{:S(2)}, u32[]{:S(2)}) async-start(bf16[16,256,192]{1,2,0:T(8,128)(2,1)} %fusion.13), calls=%async_computation | async-start | bytes 3145728 | tf_op jit(solution)/shard_map/all_to_all | solution.py:102
